TPU v7x, 128 devices: a whole 4x4x4 slice. The times are simulated.
128 devices in a mesh: row: 8 (over z, core), col: 16 (over y, x).
Axes of the slice: x: 4, y: 4, z: 4, core: 2. Of those that a mesh axis runs over, the one named last changes fastest.
Arguments:
- coeffs: float32 [2048, 3, 64, 128], P(('row', 'col')), may hold values from -0.18 to 0.18
- degree: int32 [2048], P(('row', 'col')), may hold values from 16 to 63
- material: float32 [2048, 2], P(('row', 'col')), may hold values from 0.2 to 2
- split_coeffs: float32 [512, 3, 64, 64], P(('row', 'col')), may hold values from -0.18 to 0.18
- split_material: float32 [256, 2], replicated, may hold values from 0.2 to 2
- separation: float32 [3, 2048, 8], P(None, ('row', 'col')), may hold values from -2.6 to 2.6, as said below
- reader_dev: int32 [2048, 8], P(('row', 'col')), may hold values from 0 to 127, all different within a row; in each aligned block of 16 rows (0 to 15, 16 to 31, ...) at most 2 rows name the same one
- reader_slot: int32 [2048, 8], P(('row', 'col')), may hold values from 0 to 15
Outputs:
- traction_coeffs: float32 [2048, 64, 128], P(('row', 'col'))
- split_traction: float32 [512, 64, 64], P(('row', 'col'))
- near_velocity: float32 [3, 8192], P(None, ('row', 'col'))
Inputs may be any that keep to these rules, and one draw needn't show every extreme that they name: `reader_dev`: each ordinary drop names 8 different devices; among the drops of one device at most 2 name the same device, and some device is named exactly 2 times. Each entry's separation vector has a length between 1.9 and 2.6.
All inputs are finite; a program needn't handle non-finite values.
Results may differ from a plain program's by a relative error of at most 0.019.
Values may be sent and summed in bfloat16 or wider, within the bound.
No kernel may reach another device: no remote copies, remote signals or barrier semaphores. Data moves between devices by JAX's collectives and lax.ppermute only.
A program may use at most 128 MiB of HBM per device.

v0:
```python
import functools
import math

import jax
import jax.numpy as jnp
import numpy as np
from jax import lax
from jax.experimental import pallas as pl
from jax.experimental.pallas import tpu as pltpu
from jax.sharding import PartitionSpec as P

HIGH = lax.Precision.HIGHEST
SPECTRAL = lax.Precision.DEFAULT
SOFTENING = 0.04


def from_partner(block, axis, stride):
    count = lax.axis_size(axis)
    route = []
    for low in range(count):
        high = low | 1 << stride
        if high != low and high < count:
            route += [(low, high), (high, low)]
    return lax.ppermute(block, axis, route)


def spectral_tables(degrees):
    nlon = 2 * degrees
    theta_lat = (np.arange(degrees) + 0.5) * (math.pi / degrees)
    cosine = np.cos(theta_lat)
    sine_theta = np.sin(theta_lat)
    legendre = np.zeros((degrees, degrees, degrees))
    for order in range(degrees):
        log_total = 0.0
        for step_index in range(1, order + 1):
            log_total = log_total + math.log((2.0 * step_index + 1.0) / (2.0 * step_index))
        diag_value = np.exp(0.5 * log_total + order * np.log(sine_theta)) / math.sqrt(4.0 * math.pi)
        legendre[order, :, order] = diag_value
        prev_two = diag_value
        if order + 1 < degrees:
            prev_one = math.sqrt(2.0 * order + 3.0) * cosine * diag_value
            legendre[order, :, order + 1] = prev_one
            for level in range(order + 2, degrees):
                alpha_term = math.sqrt(
                    (4.0 * level * level - 1.0) / (level * level - order * order)
                )
                beta_term = math.sqrt(
                    ((level - 1.0) ** 2 - order * order) / (4.0 * (level - 1.0) ** 2 - 1.0)
                )
                current = alpha_term * (cosine * prev_one - beta_term * prev_two)
                legendre[order, :, level] = current
                prev_two = prev_one
                prev_one = current
    order_index = np.arange(degrees)
    lon_index = np.arange(nlon)
    phase_angle = order_index[:, None] * lon_index[None, :] % nlon * (2.0 * math.pi / nlon)
    fourier = np.concatenate([np.cos(phase_angle), np.sin(phase_angle)], axis=0)
    quad_weight = sine_theta * (math.pi / degrees) * (2.0 * math.pi / nlon)
    longitude = lon_index * (2.0 * math.pi / nlon)
    normals = np.stack(
        [
            sine_theta[:, None] * np.cos(longitude)[None, :],
            sine_theta[:, None] * np.sin(longitude)[None, :],
            cosine[:, None] * np.ones((1, nlon)),
        ],
        axis=0,
    )
    return (
        jnp.asarray(legendre, dtype=jnp.float32),
        jnp.asarray(fourier, dtype=jnp.float32),
        jnp.asarray(quad_weight, dtype=jnp.float32),
        jnp.asarray(normals, dtype=jnp.float32),
    )


def legendre_synth(coeff, legendre):
    batch_size, degrees, _ = coeff.shape
    orders = legendre.shape[0]
    parted = coeff.reshape(batch_size, degrees, 2, orders)
    return jnp.einsum("mjl,nlcm->njcm", legendre, parted, precision=SPECTRAL)


def fourier_synth(partial_legendre, fourier_rows):
    batch_size, nlat, two, orders = partial_legendre.shape
    return jnp.einsum(
        "njw,wk->njk",
        partial_legendre.reshape(batch_size, nlat, two * orders),
        fourier_rows,
        precision=SPECTRAL,
    )


def analysis_fourier(traction_grid, fourier, quad_weight):
    batch_size, nlat, _ = traction_grid.shape
    projected = (
        jnp.einsum("bjk,wk->bjw", traction_grid, fourier, precision=SPECTRAL)
        * quad_weight[None, :, None]
    )
    return projected.reshape(batch_size, nlat, 2, fourier.shape[0] // 2)


def analysis_legendre(coef_grid, legendre):
    batch_size = coef_grid.shape[0]
    result = jnp.einsum("mjl,bjcm->blcm", legendre, coef_grid, precision=SPECTRAL)
    return result.reshape(batch_size, legendre.shape[2], 2 * legendre.shape[0])


def prepare(coeffs, keep_mask):
    degrees = coeffs.shape[2]
    degree_value = jnp.arange(degrees, dtype=jnp.float32)
    shape_part = coeffs[:, 0] * keep_mask
    curvature = (
        shape_part * (degree_value * (degree_value + 1.0) / (degrees * degrees))[None, :, None]
    )
    electric = 3.0 * coeffs[:, 1] * keep_mask
    viscous = 3.0 * coeffs[:, 2] * keep_mask * ((degree_value + 2.0) / degrees)[None, :, None]
    return jnp.stack([shape_part, curvature, electric, viscous], axis=1)


def traction(surface, material):
    radius = jnp.exp(surface[:, 0])
    traction_grid = (
        material[:, 0, None, None] * surface[:, 1]
        + 0.5 * surface[:, 2] * surface[:, 2]
        + 2.0 * material[:, 1, None, None] * surface[:, 3]
    )
    return (radius, traction_grid)


def per_device(
    coeffs, degree, material, split_coeffs, split_material, separation, reader_dev, reader_slot
):
    drop_count, _, degrees, coef_width = coeffs.shape
    legendre, fourier, quad_weight, normals = spectral_tables(degrees)
    nlat = legendre.shape[1]
    nlon = fourier.shape[1]
    degree_index = jnp.arange(degrees, dtype=jnp.int32)
    order_full = jnp.arange(coef_width, dtype=jnp.int32) % degrees
    order_mask = (degree_index[:, None] >= order_full[None, :]).astype(jnp.float32)
    keep_mask = order_mask[None] * (degree_index[None, :, None] <= degree[:, None, None]).astype(
        jnp.float32
    )
    prepared = prepare(coeffs, keep_mask)
    partial_legendre = legendre_synth(
        prepared.reshape(drop_count * 4, degrees, coef_width), legendre
    )
    surface = fourier_synth(partial_legendre, fourier).reshape(drop_count, 4, nlat, nlon)
    radius, traction_grid = traction(surface, material)
    split_count = split_coeffs.shape[0]
    half_width = split_coeffs.shape[3]
    half_orders = half_width // 2
    half_index = lax.axis_index("row") % 2
    pair_start = (
        lax.axis_index("row") // 2 * lax.axis_size("col") + lax.axis_index("col")
    ) * split_count
    own_material = lax.dynamic_slice_in_dim(split_material, pair_start, split_count, 0)
    own_order = half_index * half_orders + jnp.arange(half_width, dtype=jnp.int32) % half_orders
    keep_half = (degree_index[:, None] >= own_order[None, :]).astype(jnp.float32)
    own_legendre = lax.dynamic_slice_in_dim(legendre, half_index * half_orders, half_orders, 0)
    own_fourier = lax.dynamic_slice_in_dim(
        fourier.reshape(2, degrees, nlon), half_index * half_orders, half_orders, 1
    ).reshape(half_width, nlon)
    split_prepared = prepare(split_coeffs, keep_half[None])
    split_legendre = legendre_synth(
        split_prepared.reshape(split_count * 4, degrees, half_width), own_legendre
    )
    partial_surface = fourier_synth(split_legendre, own_fourier)
    split_surface = partial_surface + from_partner(
        partial_surface.astype(jnp.bfloat16), "row", 0
    ).astype(partial_surface.dtype)
    _, split_grid = traction(split_surface.reshape(split_count, 4, nlat, nlon), own_material)
    near_grid = jnp.stack([radius, traction_grid], axis=1).astype(jnp.bfloat16)
    point_grid = radius[:, nlat // 4 :: nlat // 2, :: nlon // 2].astype(jnp.bfloat16)
    point_count = point_grid.shape[1] * point_grid.shape[2]
    own_points = point_grid.reshape(drop_count, point_count)
    target_normal = normals[:, nlat // 4 :: nlat // 2, :: nlon // 2].reshape(3, point_count)
    devices = lax.axis_size("row") * lax.axis_size("col")
    all_points = lax.all_to_all(
        jnp.broadcast_to(own_points.reshape(1, -1), (devices, drop_count * point_count)),
        ("row", "col"),
        split_axis=0,
        concat_axis=0,
        tiled=True,
    ).reshape(devices * drop_count, point_count)
    total_drops = all_points.shape[0]
    readers = reader_dev.shape[1]
    target = (reader_dev * drop_count + reader_slot).reshape(-1)
    pick = (target[:, None] == jnp.arange(total_drops, dtype=jnp.int32)[None, :]).astype(
        jnp.float32
    )
    target_radius = jnp.dot(pick, all_points.astype(jnp.float32), precision=HIGH)
    target_point = separation.reshape(3, drop_count * readers)[:, :, None] + (
        target_radius[None] * target_normal[:, None, :]
    )
    target_point = jnp.transpose(
        target_point.reshape(3, drop_count, readers * point_count), (1, 2, 0)
    )
    target_square = jnp.sum(target_point * target_point, axis=2) + SOFTENING
    entry_table = jnp.concatenate(
        [
            jnp.transpose(separation, (1, 2, 0)),
            target_radius.reshape(drop_count, readers, point_count),
            target_square.reshape(drop_count, readers, point_count),
        ],
        axis=2,
    ).reshape(-1)
    cell_table = cell_tables(nlat, nlon, point_count)
    partial = near_field(entry_table, near_grid, cell_table, readers, point_count)
    partial, traction_grid, split_grid = lax.optimization_barrier(
        (partial, traction_grid, split_grid)
    )
    sums = jnp.sum(partial, axis=3)
    contribution = (
        sums[:, :3] + jnp.transpose(target_point, (0, 2, 1)) * sums[:, 3:]
    ) / (8.0 * math.pi)
    contribution = jnp.transpose(
        contribution.reshape(drop_count, 3, readers, point_count), (0, 2, 1, 3)
    ).reshape(drop_count * readers, 3 * point_count)
    destination = reader_dev.reshape(-1)
    capacity = 2
    onehot = (destination[:, None] == jnp.arange(devices, dtype=jnp.int32)[None, :]).astype(
        jnp.int32
    )
    rank = jnp.sum((jnp.cumsum(onehot, axis=0) - onehot) * onehot, axis=1)
    position = destination * capacity + rank
    place = (position[:, None] == jnp.arange(devices * capacity, dtype=jnp.int32)[None, :]).astype(
        jnp.float32
    )
    record = jnp.concatenate(
        [contribution, reader_slot.reshape(-1, 1).astype(jnp.float32)], axis=1
    )
    outgoing = jnp.dot(jnp.transpose(place), record, precision=HIGH)
    incoming = lax.all_to_all(
        outgoing.reshape(devices, capacity, record.shape[1]),
        ("row", "col"),
        split_axis=0,
        concat_axis=0,
        tiled=True,
    ).reshape(devices * capacity, record.shape[1])
    slot_pick = (
        incoming[:, -1:] == jnp.arange(drop_count, dtype=jnp.float32)[None, :]
    ).astype(jnp.float32)
    mine = jnp.dot(jnp.transpose(slot_pick), incoming[:, :-1], precision=HIGH)
    near_velocity = jnp.transpose(mine.reshape(drop_count, 3, point_count), (1, 0, 2))
    traction_coeffs = (
        analysis_legendre(analysis_fourier(traction_grid, fourier, quad_weight), legendre)
        * keep_mask
    )
    coef_grid = analysis_fourier(split_grid, fourier, quad_weight)
    own_grid = lax.dynamic_slice_in_dim(coef_grid, half_index * half_orders, half_orders, 3)
    split_traction = analysis_legendre(own_grid, own_legendre) * keep_half[None]
    return (traction_coeffs, split_traction, near_velocity.reshape(3, drop_count * point_count))


def cell_tables(nlat, nlon, point_count):
    theta = (np.arange(nlat) + 0.5) * (math.pi / nlat)
    longitude = np.arange(nlon) * (2.0 * math.pi / nlon)
    quad_weight = (np.sin(theta) * (math.pi / nlat) * (2.0 * math.pi / nlon)).astype(np.float32)
    normals = np.stack(
        [
            np.sin(theta)[:, None] * np.cos(longitude)[None, :],
            np.sin(theta)[:, None] * np.sin(longitude)[None, :],
            np.cos(theta)[:, None] * np.ones((1, nlon)),
        ],
        axis=0,
    ).astype(np.float32)
    points = normals[:, nlat // 4 :: nlat // 2, :: nlon // 2].reshape(3, point_count)
    facing = np.einsum("dp,djk->pjk", points.astype(np.float64), normals.astype(np.float64))
    weight = np.broadcast_to(quad_weight[None, :, None], (1, nlat, nlon))
    table = np.concatenate([normals, facing.astype(np.float32), weight], axis=0)
    return jnp.asarray(table, dtype=jnp.float32)


def near_kernel(points, t_ref, g_ref, c_ref, o_ref, s_ref):
    drop = pl.program_id(0)
    entries = o_ref.shape[2] // points
    width = 3 + 2 * points
    chunks = g_ref.shape[2] // 8
    r = g_ref[0, 0].astype(jnp.float32)
    s_ref[0] = r
    s_ref[1] = r * r
    s_ref[2] = r + r
    s_ref[3] = g_ref[0, 1].astype(jnp.float32) * r * r * c_ref[3 + points]

    def body(e, carry):
        base = (drop * entries + e) * width
        sx = t_ref[base]
        sy = t_ref[base + 1]
        sz = t_ref[base + 2]
        lift = [t_ref[base + 3 + k] for k in range(points)]
        tt = [t_ref[base + 3 + points + k] for k in range(points)]
        acc = [[jnp.zeros((8, 128), jnp.float32) for _ in range(4)] for _ in range(points)]
        for c in range(chunks):
            rows = pl.ds(c * 8, 8)
            nx = c_ref[0, rows, :]
            ny = c_ref[1, rows, :]
            nz = c_ref[2, rows, :]
            rr = s_ref[0, rows, :]
            r2 = s_ref[1, rows, :]
            twice = s_ref[2, rows, :]
            load = s_ref[3, rows, :]
            shared = sx * nx + sy * ny + sz * nz
            for k in range(points):
                along = shared + lift[k] * c_ref[3 + k, rows, :]
                soft = (tt[k] + r2) - twice * along
                inv = lax.rsqrt(soft)
                w = load * (inv * inv * inv)
                dn = along - rr
                h = w * ((soft + SOFTENING) - dn * rr)
                hx, hy, hz, sq = acc[k]
                acc[k] = [hx + h * nx, hy + h * ny, hz + h * nz, sq + w * dn]
        for k in range(points):
            row = pl.ds(e * points + k, 1)
            for comp in range(4):
                o_ref[0, comp, row, :] = jnp.sum(acc[k][comp], axis=0, keepdims=True)
        return carry

    lax.fori_loop(0, entries, body, 0)


def near_field(entry_table, near_grid, cell_table, readers, points):
    drops, fields, nlat, nlon = near_grid.shape
    targets = readers * points
    cells = drops * targets * nlat * nlon
    return pl.pallas_call(
        functools.partial(near_kernel, points),
        grid=(drops,),
        in_specs=[
            pl.BlockSpec(memory_space=pltpu.SMEM),
            pl.BlockSpec((1, fields, nlat, nlon), lambda s: (s, 0, 0, 0)),
            pl.BlockSpec(cell_table.shape, lambda s: (0, 0, 0)),
        ],
        out_specs=pl.BlockSpec((1, 4, targets, nlon), lambda s: (s, 0, 0, 0)),
        out_shape=jax.ShapeDtypeStruct((drops, 4, targets, nlon), jnp.float32),
        scratch_shapes=[pltpu.VMEM((4, nlat, nlon), jnp.float32)],
        cost_estimate=pl.CostEstimate(
            flops=24 * cells, transcendentals=cells, bytes_accessed=2 * drops * fields * nlat * nlon
        ),
    )(entry_table, near_grid, cell_table)


def solution(mesh):
    in_specs = (
        P(("row", "col"), None, None, None),
        P(("row", "col")),
        P(("row", "col"), None),
        P(("row", "col"), None, None, None),
        P(),
        P(None, ("row", "col"), None),
        P(("row", "col"), None),
        P(("row", "col"), None),
    )
    out_specs = (
        P(("row", "col"), None, None),
        P(("row", "col"), None, None),
        P(None, ("row", "col")),
    )
    return jax.shard_map(
        per_device, mesh=mesh, in_specs=in_specs, out_specs=out_specs, check_vma=False
    )
```

profile of v0, /device:TPU:0, one launch (start us, length us, event | category | flops | bytes accessed | tf_op | source)
XLA Modules:
  0.0 92.5 jit_solution(4745403160763043714)
XLA Ops:
  0.7 0.7 fusion.37
  1.4 1.7 %broadcast_multiply_fusion = (bf16[16,1,64,128]{3,2,1,0:T(8,128)(2,1)S(1)}, bf16[16,1,64,128]{3,2,1,0:T(8,128)(2,1)S(1)}, bf16[16,1,64,128]{3,2,1,0:T(8,128)(2,1)S(1)}, bf16[16,1,64,128]{3,2,1,0:T(8,128)(2,1)S(1)}) fusion(f32[64]{0:T(128)S(1)} %get-tuple-element.42, f32[16,64]{1,0:T(8,128)S(1)} %fusion.37, f32[64,128]{1,0:T(8,128)S(1)} %fusion.32, ...), kind=kLoop, calls=%fused_computation.38 | loop fusion | flops 1572864 | bytes 2658816 | tf_op jit(solution)/shard_map/mul | solution.py:113
  3.2 0.1 pad_maximum_fusion
  3.3 0.8 reshape_reshape.7
  4.2 4.4 %copy.127 = bf16[64,64,2,64]{1,0,2,3:T(8,128)(2,1)} copy(bf16[64,64,2,64]{3,2,1,0:T(2,128)(2,1)S(1)} %reshape_reshape.7) | data formatting | bytes 2097152 | tf_op jit(solution)/shard_map/reshape;reshape | solution.py:79
  8.6 2.3 %convolution_bitcast_fusion = bf16[64,64,2,64]{1,0,2,3:T(8,128)(2,1)S(1)} fusion(bf16[64,64,2,64]{1,0,2,3:T(8,128)(2,1)} %copy.127, bf16[64,64,64,1]{2,1,3,0:T(8,128)(2,1)S(1)} %copy-done.1), kind=kOutput, calls=%fused_computation | convolution fusion | flops 67108864 | bytes 2621440 | tf_op jit(solution)/shard_map/mjl,nlcm->njcm/dot_general | solution.py:80
  10.9 4.6 %copy.128 = bf16[64,64,2,64]{3,2,1,0:T(2,128)(2,1)} copy(bf16[64,64,2,64]{1,0,2,3:T(8,128)(2,1)S(1)} %convolution_bitcast_fusion) | data formatting | bytes 2097152 | tf_op jit(solution)/shard_map/mjl,nlcm->njcm/transpose | solution.py:80
  15.5 3.9 %dot_general.36 = bf16[16,4,64,128]{3,2,1,0:T(8,128)(2,1)S(1)} reshape(bf16[64,64,2,64]{3,2,1,0:T(2,128)(2,1)} %copy.128) | data formatting | bytes 2097152 | tf_op jit(solution)/shard_map/njw,wk->njk/dot_general | solution.py:85
  19.5 0.4 fusion.47
  19.9 0.3 fusion.8
  20.2 0.2 slice.76
  20.3 0.1 broadcast_in_dim.4
  20.5 0.7 broadcast_in_dim.5
  21.1 11.2 %all-to-all-start = ((bf16[128,1,64]{2,1,0:T(2,128)(2,1)}), bf16[128,1,64]{2,1,0:T(2,128)(2,1)S(1)}, u32[]{:S(2)}, u32[]{:S(2)}) async-start(bf16[128,1,64]{2,1,0:T(2,128)(2,1)} %broadcast_in_dim.5), calls=%async_computation | async-start | bytes 131072 | tf_op jit(solution)/shard_map/all_to_all | solution.py:178
  32.5 1.1 %fusion.44 = (f32[4,1,64,64]{3,2,1,0:T(8,128)S(1)}, f32[4,1,64,64]{3,2,1,0:T(8,128)S(1)}, f32[4,1,64,64]{3,2,1,0:T(8,128)S(1)}) fusion(f32[4,3,64,64]{3,2,1,0:T(8,128)} %param.16), kind=kLoop, calls=%fused_computation.100 | loop fusion | bytes 393216 | tf_op jit(solution)/shard_map/slice | solution.py:111
  33.6 0.1 copy.167
  33.7 0.1 copy.168
  33.8 0.1 copy.166
  34.0 1.4 %convolution_bitcast_fusion.3 = bf16[16,64,2,32]{1,0,2,3:T(8,128)(2,1)S(1)} fusion(bf16[64,64,64]{2,1,0:T(8,128)(2,1)} %constant.191, s32[]{:T(128)S(6)} %select_n.46, bf16[16,64,2,32]{1,3,2,0:T(8,128)(2,1)S(1)} %bitcast.127), kind=kOutput, calls=%fused_computation.4 | convolution fusion | flops 8388608 | bytes 786436 | tf_op jit(solution)/shard_map/mjl,nlcm->njcm/dot_general | solution.py:80
  35.5 1.7 %fusion.46 = (bf16[16,64,128]{2,1,0:T(8,128)(2,1)}, f32[16,64,128]{2,1,0:T(8,128)S(1)}) fusion(bf16[2,64,128]{2,1,0:T(8,128)(2,1)} %constant.192, s32[]{:T(128)S(6)} %select_n.46, bf16[16,64,2,32]{1,0,2,3:T(8,128)(2,1)S(1)} %convolution_bitcast_fusion.3), kind=kOutput, calls=%fused_computation.102 | convolution fusion | flops 16908288 | bytes 933892 | tf_op jit(solution)/shard_map/njw,wk->njk/dot_general | solution.py:85
  37.2 0.9 fusion.10
  38.2 0.8 fusion.45
  39.2 0.2 reduce_window_sum.11
  39.4 0.2 select_reduce_fusion
  39.6 0.5 multiply_add_fusion.2
  40.1 0.8 pad_maximum_fusion.1.g_ref
  40.9 0.8 copy.125
  41.7 0.1 add.129
  41.8 0.1 add.130
  41.9 0.1 add.131
  42.1 0.7 mul.335
  42.8 0.1 mul.336
  43.2 0.2 reduce.1
  43.4 0.6 reshape.231
  44.0 0.4 fusion.4
  44.4 0.1 copy.130
  44.9 0.2 copy.133
  45.1 0.8 reshape.233.t_ref
  45.9 18.2 %shard_map.148 = f32[16,4,32,128]{3,2,1,0:T(8,128)} custom-call(f32[1408]{0:T(1024)} %reshape.233.t_ref, bf16[16,2,64,128]{3,2,1,0:T(8,128)(2,1)} %pad_maximum_fusion.1.g_ref, f32[8,64,128]{2,1,0:T(8,128)} %constant.116.clone.c_ref), custom_call_target="tpu_custom_call" | custom-call | flops 100663296 | bytes 524288 | tf_op jit(solution)/shard_map/pallas_call | solution.py:325
  64.0 1.1 %convert_add_fusion = f32[16,64,128]{2,1,0:T(8,128)S(1)} fusion(f32[16,64,128]{2,1,0:T(8,128)S(1)} %get-tuple-element.41, bf16[16,64,128]{2,1,0:T(8,128)(2,1)} %collective-permute-done), kind=kLoop, calls=%fused_computation.36 | loop fusion | flops 262144 | bytes 1310720 | tf_op jit(solution)/shard_map/add | solution.py:168
  65.1 0.1 fusion.17
  65.3 0.2 convolution_multiply_fusion
  65.5 0.2 reshape.236
  65.7 0.7 copy.145
  66.4 0.4 convolution_bitcast_fusion.1
  66.8 0.7 copy.146
  67.5 0.6 reshape.237
  68.1 1.0 %multiply_multiply_fusion.5 = f32[16,64,128]{2,1,0:T(8,128)} fusion(f32[16,64,128]{2,1,0:T(8,128)S(1)} %reshape.237, f32[16,64]{1,0:T(8,128)S(1)} %fusion.37, f32[64,128]{1,0:T(8,128)S(1)} %fusion.32), kind=kLoop, calls=%fused_computation.35 | loop fusion | flops 262144 | bytes 1085440 | tf_op jit(solution)/shard_map/mul | solution.py:246
  69.1 0.2 convolution_multiply_fusion.1
  69.3 0.1 reshape.238
  69.4 0.2 constant_dynamic-slice_fusion
  69.6 0.1 copy.172
  69.8 0.3 convolution_bitcast_fusion.4
  70.1 0.4 reduce_sum.29
  70.6 0.1 copy.152
  70.7 0.1 reshape.242
  70.8 1.0 %fusion.23 = f32[256,13]{1,0:T(8,128)} fusion(s32[128]{0:T(128)S(1)} %copy-done.14, f32[128,1]{0,1:T(1,128)S(1)} %convert_element_type.60, f32[128,12]{0,1:T(8,128)S(1)} %reshape.242), kind=kOutput, calls=%fused_computation.56 | convolution fusion | flops 5179008 | bytes 20480 | tf_op jit(solution)/shard_map/dot_general | solution.py:232
  71.8 9.9 %all-to-all-start.1 = ((f32[128,2,13]{2,1,0:T(2,128)}), f32[128,2,13]{2,1,0:T(2,128)S(1)}, u32[]{:S(2)}, u32[]{:S(2)}) async-start(f32[128,2,13]{2,1,0:T(2,128)} %bitcast.36), calls=%async_computation.1 | async-start | bytes 262144 | tf_op jit(solution)/shard_map/all_to_all | solution.py:233
  81.7 0.8 copy.157
  82.4 8.8 %all-to-all-done.1 = f32[128,2,13]{2,1,0:T(2,128)S(1)} async-done(((f32[128,2,13]{2,1,0:T(2,128)}), f32[128,2,13]{2,1,0:T(2,128)S(1)}, u32[]{:S(2)}, u32[]{:S(2)}) %all-to-all-start.1) | async-done | bytes 13344 | tf_op jit(solution)/shard_map/all_to_all | solution.py:233
  91.2 0.2 slice_reduce_fusion
  91.4 0.3 fusion.18
  91.7 0.1 copy.156
  91.8 0.7 reshape.246
  (65 shorter events, 1.5 us)
Async XLA Ops:
  0.6 38.3 %copy-start = (f32[256,2]{0,1:T(2,128)S(1)}, f32[256,2]{0,1:T(2,128)}, u32[]{:S(2)}) copy-start(f32[256,2]{0,1:T(2,128)} %param.17) | copy-start | bytes 6148
  0.7 2.7 %copy-start.11 = (f32[64]{0:T(128)}, f32[64]{0:T(128)S(1)}, u32[]{:S(2)}) copy-start(f32[64]{0:T(128)S(1)} %get-tuple-element.42) | copy-start | bytes 772
  4.2 4.4 %copy-start.1 = (bf16[64,64,64,1]{2,1,3,0:T(8,128)(2,1)S(1)}, bf16[64,64,64,1]{2,1,3,0:T(8,128)(2,1)}, u32[]{:S(2)}) copy-start(bf16[64,64,64,1]{2,1,3,0:T(8,128)(2,1)} %constant.189) | copy-start | bytes 1572868
  15.5 3.9 %copy-start.13 = (f32[16,2]{0,1:T(2,128)S(1)}, f32[16,2]{0,1:T(2,128)}, u32[]{:S(2)}) copy-start(f32[16,2]{0,1:T(2,128)} %param.15) | copy-start | bytes 388
  15.5 3.9 %copy-start.6 = (bf16[128,128,1,1]{1,0,3,2:T(8,128)(2,1)S(1)}, bf16[128,128,1,1]{1,0,3,2:T(8,128)(2,1)}, u32[]{:S(2)}) copy-start(bf16[128,128,1,1]{1,0,3,2:T(8,128)(2,1)} %constant.190) | copy-start | bytes 98308
  19.4 0.7 copy-start.8
  19.4 0.7 copy-start.9
  19.9 14.0 %copy-start.12 = (f32[64]{0:T(128)S(1)}, f32[64]{0:T(128)}, u32[]{:S(2)}) copy-start(f32[64]{0:T(128)} %copy-done.11) | copy-start | bytes 772
  21.1 22.1 %all-to-all-start = ((bf16[128,1,64]{2,1,0:T(2,128)(2,1)}), bf16[128,1,64]{2,1,0:T(2,128)(2,1)S(1)}, u32[]{:S(2)}, u32[]{:S(2)}) async-start(bf16[128,1,64]{2,1,0:T(2,128)(2,1)} %broadcast_in_dim.5), calls=%async_computation | async-start | bytes 131072 | tf_op jit(solution)/shard_map/all_to_all | solution.py:178
  34.0 4.1 %copy-start.7 = (s32[16,8]{0,1:T(8,128)S(1)}, s32[16,8]{0,1:T(8,128)}, u32[]{:S(2)}) copy-start(s32[16,8]{0,1:T(8,128)} %param.19) | copy-start | bytes 1540
  37.2 26.8 %collective-permute-start = (bf16[16,64,128]{2,1,0:T(8,128)(2,1)}, bf16[16,64,128]{2,1,0:T(8,128)(2,1)}, u32[]{:S(2)}, u32[]{:S(2)}) collective-permute-start(bf16[16,64,128]{2,1,0:T(8,128)(2,1)} %get-tuple-element.40), channel_id=1, source_target_pairs={{0,16},{16,0},{32,48},{48,32},{64,80},{80,64},{96,112},{112,96},{1... | collective-permute-start | bytes 786440 | tf_op jit(solution)/shard_map/ppermute | solution.py:24
  45.9 19.4 %copy-start.5 = (bf16[128,128,1]{1,0,2:T(8,128)(2,1)S(1)}, bf16[128,128,1]{1,0,2:T(8,128)(2,1)}, u32[]{:S(2)}) copy-start(bf16[128,128,1]{1,0,2:T(8,128)(2,1)} %constant.193) | copy-start | bytes 98308
  45.9 19.4 %copy-start.10 = (f32[64]{0:T(128)S(1)}, f32[64]{0:T(128)}, u32[]{:S(2)}) copy-start(f32[64]{0:T(128)} %constant.114.clone) | copy-start | bytes 772
  64.0 2.4 %copy-start.2 = (bf16[64,64,64,1]{2,1,3,0:T(8,128)(2,1)S(1)}, bf16[64,64,64,1]{2,1,3,0:T(8,128)(2,1)}, u32[]{:S(2)}) copy-start(bf16[64,64,64,1]{2,1,3,0:T(8,128)(2,1)} %constant.189) | copy-start | bytes 1572868
  67.5 2.3 %copy-start.3 = (bf16[64,64,64]{2,1,0:T(8,128)(2,1)S(1)}, bf16[64,64,64]{2,1,0:T(8,128)(2,1)}, u32[]{:S(2)}) copy-start(bf16[64,64,64]{2,1,0:T(8,128)(2,1)} %constant.191) | copy-start | bytes 1572868
  68.1 2.0 %copy-start.4 = (f32[16,4,32,128]{3,2,1,0:T(8,128)S(1)}, f32[16,4,32,128]{3,2,1,0:T(8,128)}, u32[]{:S(2)}) copy-start(f32[16,4,32,128]{3,2,1,0:T(8,128)} %shard_map.148) | copy-start | bytes 3145732
  68.1 2.7 %copy-start.14 = (s32[128]{0:T(128)S(1)}, s32[128]{0:T(128)}, u32[]{:S(2)}) copy-start(s32[128]{0:T(128)} %multiply_add_fusion.2) | copy-start | bytes 1540
  71.8 19.5 %all-to-all-start.1 = ((f32[128,2,13]{2,1,0:T(2,128)}), f32[128,2,13]{2,1,0:T(2,128)S(1)}, u32[]{:S(2)}, u32[]{:S(2)}) async-start(f32[128,2,13]{2,1,0:T(2,128)} %bitcast.36), calls=%async_computation.1 | async-start | bytes 262144 | tf_op jit(solution)/shard_map/all_to_all | solution.py:233
where the time goes:
time: 93.9 us; the launch traced here: 92.5 us
  local copies, waits for them, and re-layouts  25.3 us (27%)
  starting transfers between devices  21 us (22%)
  Pallas kernels  18.2 us (19%)
  other arithmetic  9.43 us (10%)
  waiting for transfers between devices  8.8 us (9%)
  matrix products  8.57 us (9%)
  between operations  1.23 us (1%)
    pallas_call x1, Pallas kernels, near_field(): pl.pallas_call(functools.partial(near_kernel, points), grid=(drops,), in_...  18.2 us
    all_to_all x1, starting transfers between devices, per_device(): lax.all_to_all(jnp.broadcast_to(own_points.reshape(1, -1), (devices, drop...  11.2 us
    all_to_all x1, starting transfers between devices, per_device(): lax.all_to_all(outgoing.reshape(devices, capacity, record.shape[1]), ('ro...  9.87 us
    all_to_all x1, waiting for transfers between devices, per_device(): lax.all_to_all(outgoing.reshape(devices, capacity, record.shape[1]), ('ro...  8.79 us
    another operation x2, local copies, waits for them, and re-layouts, legendre_synth(): parted = coeff.reshape(batch_size, degrees, 2, orders)  5.22 us
    transpose x1, local copies, waits for them, and re-layouts, legendre_synth(): return jnp.einsum('mjl,nlcm->njcm', legendre, parted, precision=SPECTRAL)  4.62 us
    dot_general x1, local copies, waits for them, and re-layouts, fourier_synth(): jnp.einsum('njw,wk->njk', partial_legendre.reshape(batch_size, nlat, two...  3.9 us
    dot_general x2, matrix products, legendre_synth(): return jnp.einsum('mjl,nlcm->njcm', legendre, parted, precision=SPECTRAL)  3.74 us
  transfers between devices with their start and end apart: 3, of which 1 were waited for; matrix products, arithmetic and copies ran while one was open for 15% of the time, Pallas kernels for 20%

commit v1 on v0

--- a/solution.py
+++ b/solution.py
@@ -73,6 +73,55 @@
     )
 
 
+def spectral_tables_np(degrees):
+    nlon = 2 * degrees
+    theta_lat = (np.arange(degrees) + 0.5) * (math.pi / degrees)
+    cosine = np.cos(theta_lat)
+    sine_theta = np.sin(theta_lat)
+    legendre = np.zeros((degrees, degrees, degrees))
+    for order in range(degrees):
+        log_total = 0.0
+        for step_index in range(1, order + 1):
+            log_total = log_total + math.log((2.0 * step_index + 1.0) / (2.0 * step_index))
+        diag_value = np.exp(0.5 * log_total + order * np.log(sine_theta)) / math.sqrt(4.0 * math.pi)
+        legendre[order, :, order] = diag_value
+        prev_two = diag_value
+        if order + 1 < degrees:
+            prev_one = math.sqrt(2.0 * order + 3.0) * cosine * diag_value
+            legendre[order, :, order + 1] = prev_one
+            for level in range(order + 2, degrees):
+                alpha_term = math.sqrt(
+                    (4.0 * level * level - 1.0) / (level * level - order * order)
+                )
+                beta_term = math.sqrt(
+                    ((level - 1.0) ** 2 - order * order) / (4.0 * (level - 1.0) ** 2 - 1.0)
+                )
+                current = alpha_term * (cosine * prev_one - beta_term * prev_two)
+                legendre[order, :, level] = current
+                prev_two = prev_one
+                prev_one = current
+    order_index = np.arange(degrees)
+    lon_index = np.arange(nlon)
+    phase_angle = order_index[:, None] * lon_index[None, :] % nlon * (2.0 * math.pi / nlon)
+    fourier = np.concatenate([np.cos(phase_angle), np.sin(phase_angle)], axis=0)
+    quad_weight = sine_theta * (math.pi / degrees) * (2.0 * math.pi / nlon)
+    longitude = lon_index * (2.0 * math.pi / nlon)
+    normals = np.stack(
+        [
+            sine_theta[:, None] * np.cos(longitude)[None, :],
+            sine_theta[:, None] * np.sin(longitude)[None, :],
+            cosine[:, None] * np.ones((1, nlon)),
+        ],
+        axis=0,
+    )
+    return (
+        legendre.astype(np.float32),
+        fourier.astype(np.float32),
+        quad_weight.astype(np.float32),
+        normals.astype(np.float32),
+    )
+
+
 def legendre_synth(coeff, legendre):
     batch_size, degrees, _ = coeff.shape
     orders = legendre.shape[0]
@@ -141,6 +190,11 @@
         jnp.float32
     )
     prepared = prepare(coeffs, keep_mask)
+    point_weight = point_table(degrees)
+    point_surface = jnp.dot(
+        prepared[:, 0].reshape(drop_count, degrees * coef_width), point_weight, precision=HIGH
+    )
+    own_points = jnp.exp(point_surface).astype(jnp.bfloat16)
     partial_legendre = legendre_synth(
         prepared.reshape(drop_count * 4, degrees, coef_width), legendre
     )
@@ -170,9 +224,7 @@
     ).astype(partial_surface.dtype)
     _, split_grid = traction(split_surface.reshape(split_count, 4, nlat, nlon), own_material)
     near_grid = jnp.stack([radius, traction_grid], axis=1).astype(jnp.bfloat16)
-    point_grid = radius[:, nlat // 4 :: nlat // 2, :: nlon // 2].astype(jnp.bfloat16)
-    point_count = point_grid.shape[1] * point_grid.shape[2]
-    own_points = point_grid.reshape(drop_count, point_count)
+    point_count = 4
     target_normal = normals[:, nlat // 4 :: nlat // 2, :: nlon // 2].reshape(3, point_count)
     devices = lax.axis_size("row") * lax.axis_size("col")
     all_points = lax.all_to_all(
@@ -250,6 +302,20 @@
     own_grid = lax.dynamic_slice_in_dim(coef_grid, half_index * half_orders, half_orders, 3)
     split_traction = analysis_legendre(own_grid, own_legendre) * keep_half[None]
     return (traction_coeffs, split_traction, near_velocity.reshape(3, drop_count * point_count))
+
+
+def point_table(degrees):
+    legendre, fourier, _, _ = (np.asarray(t) for t in spectral_tables_np(degrees))
+    lat = np.arange(degrees // 4, degrees, degrees // 2)
+    lon = np.arange(0, 2 * degrees, degrees)
+    orders = np.arange(2 * degrees) % degrees
+    table = np.zeros((degrees, 2 * degrees, lat.size * lon.size))
+    for i, j in enumerate(lat):
+        for k, col in enumerate(lon):
+            table[:, :, i * lon.size + k] = (
+                legendre[orders, j, :].T.astype(np.float64) * fourier[:, col][None, :]
+            )
+    return jnp.asarray(table.reshape(degrees * 2 * degrees, -1), dtype=jnp.float32)
 
 
 def cell_tables(nlat, nlon, point_count):

time: 93.9 us -> 90.7 us (0.966)
  other arithmetic: 9.43 us -> 6.22 us
    dot_general x0 -> x1, matrix products: none -> 2.32 us  [per_device(): jnp.dot(prepared[:, 0].reshape(drop_count, degrees * coef_width), point_w...]
    dot_general x2, matrix products: 3.74 us -> 2.69 us  [legendre_synth(): return jnp.einsum('mjl,nlcm->njcm', legendre, parted, precision=SPECTRAL)]
    add x1, other arithmetic: 1.1 us -> 0.06 us  [per_device(): partial_surface + from_partner(partial_surface.astype(jnp.bfloat16), 'row...]
    unnamed x37 -> x57, local copies, waits for them, and re-layouts: 2.1 us -> 2.09 us
  transfers between devices with their start and end apart: 3 -> 3, of which waited for: 1 -> 1; matrix products, arithmetic and copies ran while one was open for 15% -> 29% of each run, Pallas kernels for 20% -> 20%
where the time goes in v1:
time: 90.7 us; the launch traced here: 89.5 us
  local copies, waits for them, and re-layouts  24.6 us (27%)
  starting transfers between devices  21.1 us (23%)
  Pallas kernels  18.2 us (20%)
  matrix products  9.27 us (10%)
  waiting for transfers between devices  8.79 us (10%)
  other arithmetic  6.22 us (7%)
  between operations  1.36 us (1%)
    pallas_call x1, Pallas kernels, near_field(): pl.pallas_call(functools.partial(near_kernel, points), grid=(drops,), in_...  18.2 us
    all_to_all x1, starting transfers between devices, per_device(): lax.all_to_all(jnp.broadcast_to(own_points.reshape(1, -1), (devices, drop...  11.2 us
    all_to_all x1, starting transfers between devices, per_device(): lax.all_to_all(outgoing.reshape(devices, capacity, record.shape[1]), ('ro...  9.88 us
    all_to_all x1, waiting for transfers between devices, per_device(): lax.all_to_all(outgoing.reshape(devices, capacity, record.shape[1]), ('ro...  8.78 us
    another operation x2, local copies, waits for them, and re-layouts, legendre_synth(): parted = coeff.reshape(batch_size, degrees, 2, orders)  5.22 us
    transpose x1, local copies, waits for them, and re-layouts, legendre_synth(): return jnp.einsum('mjl,nlcm->njcm', legendre, parted, precision=SPECTRAL)  4.53 us
    dot_general x1, local copies, waits for them, and re-layouts, fourier_synth(): jnp.einsum('njw,wk->njk', partial_legendre.reshape(batch_size, nlat, two...  3.9 us
    dot_general x2, matrix products, legendre_synth(): return jnp.einsum('mjl,nlcm->njcm', legendre, parted, precision=SPECTRAL)  2.69 us
  transfers between devices with their start and end apart: 3, of which 1 were waited for; matrix products, arithmetic and copies ran while one was open for 29% of the time, Pallas kernels for 20%

profile of v1, /device:TPU:0, one launch (start us, length us, event | category | flops | bytes accessed | tf_op | source)
XLA Modules:
  0.0 89.5 jit_solution(17923336127909723570)
XLA Ops:
  0.7 0.8 fusion.45
  1.4 1.1 %slice.68 = f32[16,1,64,128]{3,2,1,0:T(8,128)S(1)} slice(f32[16,3,64,128]{3,2,1,0:T(8,128)} %param.14), slice={[0:16], [0:1], [0:64], [0:128]} | slice | bytes 1048576 | tf_op jit(solution)/shard_map/slice | solution.py:160
  2.5 0.2 mul.330
  2.8 2.3 %fusion = bf16[16,4]{0,1:T(4,128)(2,1)S(1)} fusion(f32[8192,4]{0,1:T(4,128)} %constant.118.clone, f32[2,8,64,128]{3,2,1,0:T(8,128)S(1)} %bitcast.139, f32[2,8,64,128]{3,2,1,0:T(8,128)S(1)} %bitcast.138, f32[8192]{0:T(1024)S(1)} %get-tuple-element.44), kind=kOutput, calls=%fused_computation.9 | convolution fusion | flops 6553664 | bytes 1212544 | tf_op jit(solution)/shard_map/dot_general | solution.py:194
  5.1 0.1 copy.168
  5.2 0.1 broadcast_in_dim.4
  5.3 0.7 broadcast_in_dim.5
  6.0 11.2 %all-to-all-start = ((bf16[128,1,64]{2,1,0:T(2,128)(2,1)}), bf16[128,1,64]{2,1,0:T(2,128)(2,1)S(1)}, u32[]{:S(2)}, u32[]{:S(2)}) async-start(bf16[128,1,64]{2,1,0:T(2,128)(2,1)} %broadcast_in_dim.5), calls=%async_computation | async-start | bytes 131072 | tf_op jit(solution)/shard_map/all_to_all | solution.py:230
  17.4 0.1 copy.209
  17.5 0.1 copy.210
  17.6 0.1 copy.208
  17.9 0.4 convolution_bitcast_fusion.3
  18.3 1.2 %fusion.54 = (bf16[16,64,128]{2,1,0:T(8,128)(2,1)}, f32[16,64,128]{2,1,0:T(8,128)}) fusion(bf16[2,64,128]{2,1,0:T(8,128)(2,1)S(1)} %copy-done.18, s32[]{:T(128)S(6)} %select_n.48, bf16[16,64,2,32]{1,0,2,3:T(8,128)(2,1)S(1)} %convolution_bitcast_fusion.3), kind=kOutput, calls=%fused_computation.111 | convolution fusion | flops 16908288 | bytes 1064964 | tf_op jit(solution)/shard_map/njw,wk->njk/dot_general | solution.py:134
  19.5 1.0 %broadcast_multiply_fusion = (bf16[16,1,64,128]{3,2,1,0:T(8,128)(2,1)S(1)}, bf16[16,1,64,128]{3,2,1,0:T(8,128)(2,1)S(1)}, bf16[16,1,64,128]{3,2,1,0:T(8,128)(2,1)S(1)}, bf16[16,1,64,128]{3,2,1,0:T(8,128)(2,1)S(1)}) fusion(f32[64]{0:T(128)S(1)} %get-tuple-element.47, f32[16,64]{1,0:T(8,128)S(1)} %fusion.45, f32[64,128]{1,0:T(8,128)S(1)} %get-tuple-element.43, ...), kind=kLoop, calls=%fused_computation.45 | loop fusion | flops 1572864 | bytes 2658816 | tf_op jit(solution)/shard_map/mul | solution.py:162
  20.4 0.1 pad_maximum_fusion
  20.6 0.8 reshape_reshape.6
  21.4 4.4 %copy.174 = bf16[64,64,2,64]{1,0,2,3:T(8,128)(2,1)} copy(bf16[64,64,2,64]{3,2,1,0:T(2,128)(2,1)S(1)} %reshape_reshape.6) | data formatting | bytes 2097152 | tf_op jit(solution)/shard_map/reshape;reshape | solution.py:128
  25.8 2.3 %convolution_bitcast_fusion = bf16[64,64,2,64]{1,0,2,3:T(8,128)(2,1)S(1)} fusion(bf16[64,64,2,64]{1,0,2,3:T(8,128)(2,1)} %copy.174, bf16[64,64,64,1]{2,1,3,0:T(8,128)(2,1)S(1)} %copy-done.1), kind=kOutput, calls=%fused_computation | convolution fusion | flops 67108864 | bytes 2621440 | tf_op jit(solution)/shard_map/mjl,nlcm->njcm/dot_general | solution.py:129
  28.1 4.5 %copy.175 = bf16[64,64,2,64]{3,2,1,0:T(2,128)(2,1)} copy(bf16[64,64,2,64]{1,0,2,3:T(8,128)(2,1)S(1)} %convolution_bitcast_fusion) | data formatting | bytes 2097152 | tf_op jit(solution)/shard_map/mjl,nlcm->njcm/transpose | solution.py:129
  32.7 3.9 %dot_general.41 = bf16[16,4,64,128]{3,2,1,0:T(8,128)(2,1)S(1)} reshape(bf16[64,64,2,64]{3,2,1,0:T(2,128)(2,1)} %copy.175) | data formatting | bytes 2097152 | tf_op jit(solution)/shard_map/njw,wk->njk/dot_general | solution.py:134
  36.6 0.4 fusion.55
  37.0 0.3 fusion.18
  37.3 0.2 fusion.11
  37.5 0.2 copy-done.16
  38.1 0.2 reduce_window_sum.11
  38.2 0.2 select_reduce_fusion
  38.4 0.5 multiply_add_fusion.2
  38.9 0.8 pad_maximum_fusion.1.g_ref
  39.9 0.1 add.129
  39.9 0.1 add.130
  40.1 0.1 add.131
  40.2 0.1 mul.338
  40.7 0.2 reduce.1
  40.9 0.6 reshape.238
  41.5 0.4 fusion.5
  41.9 0.1 copy.170
  42.3 0.5 copy-done.13
  42.9 0.2 copy.173
  43.0 0.8 reshape.240.t_ref
  43.8 18.2 %shard_map.157 = f32[16,4,32,128]{3,2,1,0:T(8,128)} custom-call(f32[1408]{0:T(1024)} %reshape.240.t_ref, bf16[16,2,64,128]{3,2,1,0:T(8,128)(2,1)} %pad_maximum_fusion.1.g_ref, f32[8,64,128]{2,1,0:T(8,128)} %constant.119.clone.c_ref), custom_call_target="tpu_custom_call" | custom-call | flops 100663296 | bytes 524288 | tf_op jit(solution)/shard_map/pallas_call | solution.py:391
  62.1 0.1 fusion.24
  62.2 0.2 convolution_multiply_fusion
  62.5 0.2 reshape.243
  62.7 0.7 copy.187
  63.4 0.4 convolution_bitcast_fusion.1
  63.8 0.7 copy.188
  64.5 0.6 reshape.244
  65.1 1.0 %multiply_multiply_fusion.5 = f32[16,64,128]{2,1,0:T(8,128)} fusion(f32[16,64,128]{2,1,0:T(8,128)S(1)} %reshape.244, f32[64,128]{1,0:T(8,128)S(1)} %get-tuple-element.43, f32[16,64]{1,0:T(8,128)S(1)} %fusion.45), kind=kLoop, calls=%fused_computation.42 | loop fusion | flops 262144 | bytes 1085440 | tf_op jit(solution)/shard_map/mul | solution.py:298
  66.1 0.2 convolution_multiply_fusion.1
  66.3 0.1 reshape.245
  66.4 0.2 constant_dynamic-slice_fusion
  66.6 0.1 copy.214
  66.8 0.3 convolution_bitcast_fusion.4
  67.1 0.4 reduce_sum.29
  67.6 0.1 copy.194
  67.7 0.1 reshape.249
  67.8 1.0 %fusion.30 = f32[256,13]{1,0:T(8,128)} fusion(s32[128]{0:T(128)S(1)} %copy-done.24, f32[128,1]{0,1:T(1,128)S(1)} %convert_element_type.71, f32[128,12]{0,1:T(8,128)S(1)} %reshape.249), kind=kOutput, calls=%fused_computation.64 | convolution fusion | flops 5179008 | bytes 20480 | tf_op jit(solution)/shard_map/dot_general | solution.py:284
  68.8 9.9 %all-to-all-start.1 = ((f32[128,2,13]{2,1,0:T(2,128)}), f32[128,2,13]{2,1,0:T(2,128)S(1)}, u32[]{:S(2)}, u32[]{:S(2)}) async-start(f32[128,2,13]{2,1,0:T(2,128)} %bitcast.36), calls=%async_computation.1 | async-start | bytes 262144 | tf_op jit(solution)/shard_map/all_to_all | solution.py:285
  78.7 0.8 copy.199
  79.5 8.8 %all-to-all-done.1 = f32[128,2,13]{2,1,0:T(2,128)S(1)} async-done(((f32[128,2,13]{2,1,0:T(2,128)}), f32[128,2,13]{2,1,0:T(2,128)S(1)}, u32[]{:S(2)}, u32[]{:S(2)}) %all-to-all-start.1) | async-done | bytes 13344 | tf_op jit(solution)/shard_map/all_to_all | solution.py:285
  88.2 0.2 slice_reduce_fusion
  88.4 0.3 fusion.25
  88.7 0.1 copy.198
  88.8 0.7 reshape.253
  (88 shorter events, 1.8 us)
Async XLA Ops:
  0.6 37.2 %copy-start = (f32[256,2]{0,1:T(2,128)S(1)}, f32[256,2]{0,1:T(2,128)}, u32[]{:S(2)}) copy-start(f32[256,2]{0,1:T(2,128)} %param.18) | copy-start | bytes 6148
  0.6 16.7 %copy-start.7 = (f32[4,3,64,64]{3,2,1,0:T(8,128)S(1)}, f32[4,3,64,64]{3,2,1,0:T(8,128)}, u32[]{:S(2)}) copy-start(f32[4,3,64,64]{3,2,1,0:T(8,128)} %param.17) | copy-start | bytes 589828
  2.7 15.1 %copy-start.4 = (bf16[64,64,64]{2,1,0:T(8,128)(2,1)S(1)}, bf16[64,64,64]{2,1,0:T(8,128)(2,1)}, u32[]{:S(2)}) copy-start(bf16[64,64,64]{2,1,0:T(8,128)(2,1)} %constant.201) | copy-start | bytes 1572868
  5.3 13.0 %copy-start.18 = (bf16[2,64,128]{2,1,0:T(8,128)(2,1)S(1)}, bf16[2,64,128]{2,1,0:T(8,128)(2,1)}, u32[]{:S(2)}) copy-start(bf16[2,64,128]{2,1,0:T(8,128)(2,1)} %constant.202) | copy-start | bytes 98308
  6.0 34.7 %all-to-all-start = ((bf16[128,1,64]{2,1,0:T(2,128)(2,1)}), bf16[128,1,64]{2,1,0:T(2,128)(2,1)S(1)}, u32[]{:S(2)}, u32[]{:S(2)}) async-start(bf16[128,1,64]{2,1,0:T(2,128)(2,1)} %broadcast_in_dim.5), calls=%async_computation | async-start | bytes 131072 | tf_op jit(solution)/shard_map/all_to_all | solution.py:230
  17.2 2.3 %copy-start.22 = (f32[64]{0:T(128)}, f32[64]{0:T(128)S(1)}, u32[]{:S(2)}) copy-start(f32[64]{0:T(128)S(1)} %get-tuple-element.48) | copy-start | bytes 772
  17.4 2.1 %copy-start.2 = (f32[16,3,64,128]{3,2,1,0:T(8,128)S(1)}, f32[16,3,64,128]{3,2,1,0:T(8,128)}, u32[]{:S(2)}) copy-start(f32[16,3,64,128]{3,2,1,0:T(8,128)} %param.14) | copy-start | bytes 4718596
  19.4 42.6 %collective-permute-start = (bf16[16,64,128]{2,1,0:T(8,128)(2,1)}, bf16[16,64,128]{2,1,0:T(8,128)(2,1)S(1)}, u32[]{:S(2)}, u32[]{:S(2)}) collective-permute-start(bf16[16,64,128]{2,1,0:T(8,128)(2,1)} %get-tuple-element.45), channel_id=1, source_target_pairs={{0,16},{16,0},{32,48},{48,32},{64,80},{80,64},{96,112},{112,96},{1... | collective-permute-start | bytes 786440 | tf_op jit(solution)/shard_map/ppermute | solution.py:24
  21.4 4.4 %copy-start.1 = (bf16[64,64,64,1]{2,1,3,0:T(8,128)(2,1)S(1)}, bf16[64,64,64,1]{2,1,3,0:T(8,128)(2,1)}, u32[]{:S(2)}) copy-start(bf16[64,64,64,1]{2,1,3,0:T(8,128)(2,1)} %constant.199) | copy-start | bytes 1572868
  32.7 3.9 %copy-start.23 = (f32[16,2]{0,1:T(2,128)S(1)}, f32[16,2]{0,1:T(2,128)}, u32[]{:S(2)}) copy-start(f32[16,2]{0,1:T(2,128)} %param.16) | copy-start | bytes 388
  32.7 3.9 %copy-start.15 = (bf16[128,128,1,1]{1,0,3,2:T(8,128)(2,1)S(1)}, bf16[128,128,1,1]{1,0,3,2:T(8,128)(2,1)}, u32[]{:S(2)}) copy-start(bf16[128,128,1,1]{1,0,3,2:T(8,128)(2,1)} %constant.200) | copy-start | bytes 98308
  37.0 0.7 copy-start.16
  37.0 0.8 copy-start.19
  37.3 2.5 %copy-start.17 = (f32[3,16,8]{1,2,0:T(8,128)S(1)}, f32[3,16,8]{1,2,0:T(8,128)}, u32[]{:S(2)}) copy-start(f32[3,16,8]{1,2,0:T(8,128)} %param.19) | copy-start | bytes 4612
  37.3 2.9 %copy-start.20 = (f32[3,4]{1,0:T(4,128)S(1)}, f32[3,4]{1,0:T(4,128)}, u32[]{:S(2)}) copy-start(f32[3,4]{1,0:T(4,128)} %constant.128) | copy-start | bytes 148
  40.2 21.8 %copy-start.8 = (f32[3,16,32]{2,1,0:T(8,128)}, f32[3,16,32]{2,1,0:T(8,128)S(1)}, u32[]{:S(2)}) copy-start(f32[3,16,32]{2,1,0:T(8,128)S(1)} %add.131) | copy-start | bytes 18436
  40.4 21.7 %copy-start.10 = (f32[3,16,32]{2,1,0:T(8,128)}, f32[3,16,32]{2,1,0:T(8,128)S(1)}, u32[]{:S(2)}) copy-start(f32[3,16,32]{2,1,0:T(8,128)S(1)} %mul.338) | copy-start | bytes 18436
  42.2 0.6 copy-start.13
  43.8 18.2 %copy-start.3 = (f32[16,64,128]{2,1,0:T(8,128)S(1)}, f32[16,64,128]{2,1,0:T(8,128)}, u32[]{:S(2)}) copy-start(f32[16,64,128]{2,1,0:T(8,128)} %get-tuple-element.46) | copy-start | bytes 1572868
  43.8 18.4 %copy-start.12 = (bf16[128,128,1]{1,0,2:T(8,128)(2,1)S(1)}, bf16[128,128,1]{1,0,2:T(8,128)(2,1)}, u32[]{:S(2)}) copy-start(bf16[128,128,1]{1,0,2:T(8,128)(2,1)} %constant.203) | copy-start | bytes 98308
  43.8 18.4 %copy-start.21 = (f32[64]{0:T(128)S(1)}, f32[64]{0:T(128)}, u32[]{:S(2)}) copy-start(f32[64]{0:T(128)} %constant.116.clone) | copy-start | bytes 772
  64.5 2.3 %copy-start.5 = (bf16[64,64,64]{2,1,0:T(8,128)(2,1)S(1)}, bf16[64,64,64]{2,1,0:T(8,128)(2,1)}, u32[]{:S(2)}) copy-start(bf16[64,64,64]{2,1,0:T(8,128)(2,1)} %constant.201) | copy-start | bytes 1572868
  65.1 2.0 %copy-start.6 = (f32[16,4,32,128]{3,2,1,0:T(8,128)S(1)}, f32[16,4,32,128]{3,2,1,0:T(8,128)}, u32[]{:S(2)}) copy-start(f32[16,4,32,128]{3,2,1,0:T(8,128)} %shard_map.157) | copy-start | bytes 3145732
  65.1 2.4 %copy-start.9 = (f32[3,16,32]{2,1,0:T(8,128)S(1)}, f32[3,16,32]{2,1,0:T(8,128)}, u32[]{:S(2)}) copy-start(f32[3,16,32]{2,1,0:T(8,128)} %copy-done.8) | copy-start | bytes 18436
  65.1 2.4 %copy-start.11 = (f32[3,16,32]{2,1,0:T(8,128)S(1)}, f32[3,16,32]{2,1,0:T(8,128)}, u32[]{:S(2)}) copy-start(f32[3,16,32]{2,1,0:T(8,128)} %copy-done.10) | copy-start | bytes 18436
  65.1 2.4 %copy-start.14 = (f32[16,32]{1,0:T(8,128)S(1)}, f32[16,32]{1,0:T(8,128)}, u32[]{:S(2)}) copy-start(f32[16,32]{1,0:T(8,128)} %copy-done.13) | copy-start | bytes 6148
  65.1 2.7 %copy-start.24 = (s32[128]{0:T(128)S(1)}, s32[128]{0:T(128)}, u32[]{:S(2)}) copy-start(s32[128]{0:T(128)} %multiply_add_fusion.2) | copy-start | bytes 1540
  68.8 19.4 %all-to-all-start.1 = ((f32[128,2,13]{2,1,0:T(2,128)}), f32[128,2,13]{2,1,0:T(2,128)S(1)}, u32[]{:S(2)}, u32[]{:S(2)}) async-start(f32[128,2,13]{2,1,0:T(2,128)} %bitcast.36), calls=%async_computation.1 | async-start | bytes 262144 | tf_op jit(solution)/shard_map/all_to_all | solution.py:285

commit v2 on v1

--- a/solution.py
+++ b/solution.py
@@ -192,7 +192,9 @@
     prepared = prepare(coeffs, keep_mask)
     point_weight = point_table(degrees)
     point_surface = jnp.dot(
-        prepared[:, 0].reshape(drop_count, degrees * coef_width), point_weight, precision=HIGH
+        prepared[:, 0].reshape(drop_count, degrees * coef_width),
+        point_weight,
+        precision=lax.Precision.HIGH,
     )
     own_points = jnp.exp(point_surface).astype(jnp.bfloat16)
     partial_legendre = legendre_synth(
@@ -258,10 +260,8 @@
     ).reshape(-1)
     cell_table = cell_tables(nlat, nlon, point_count)
     partial = near_field(entry_table, near_grid, cell_table, readers, point_count)
-    partial, traction_grid, split_grid = lax.optimization_barrier(
-        (partial, traction_grid, split_grid)
-    )
-    sums = jnp.sum(partial, axis=3)
+    partial, traction_grid = lax.optimization_barrier((partial, traction_grid))
+    sums = partial
     contribution = (
         sums[:, :3] + jnp.transpose(target_point, (0, 2, 1)) * sums[:, 3:]
     ) / (8.0 * math.pi)
@@ -337,7 +337,7 @@
     return jnp.asarray(table, dtype=jnp.float32)
 
 
-def near_kernel(points, t_ref, g_ref, c_ref, o_ref, s_ref):
+def near_kernel(points, t_ref, g_ref, c_ref, f_ref, s_ref, o_ref):
     drop = pl.program_id(0)
     entries = o_ref.shape[2] // points
     width = 3 + 2 * points
@@ -382,6 +382,8 @@
         return carry
 
     lax.fori_loop(0, entries, body, 0)
+    rows = o_ref.shape[1] * o_ref.shape[2]
+    f_ref[0] = jnp.sum(o_ref[0].reshape(rows, o_ref.shape[3]), axis=1, keepdims=True)
 
 
 def near_field(entry_table, near_grid, cell_table, readers, points):
@@ -396,13 +398,16 @@
             pl.BlockSpec((1, fields, nlat, nlon), lambda s: (s, 0, 0, 0)),
             pl.BlockSpec(cell_table.shape, lambda s: (0, 0, 0)),
         ],
-        out_specs=pl.BlockSpec((1, 4, targets, nlon), lambda s: (s, 0, 0, 0)),
-        out_shape=jax.ShapeDtypeStruct((drops, 4, targets, nlon), jnp.float32),
-        scratch_shapes=[pltpu.VMEM((4, nlat, nlon), jnp.float32)],
+        out_specs=pl.BlockSpec((1, 4 * targets, 1), lambda s: (s, 0, 0)),
+        out_shape=jax.ShapeDtypeStruct((drops, 4 * targets, 1), jnp.float32),
+        scratch_shapes=[
+            pltpu.VMEM((4, nlat, nlon), jnp.float32),
+            pltpu.VMEM((1, 4, targets, nlon), jnp.float32),
+        ],
         cost_estimate=pl.CostEstimate(
             flops=24 * cells, transcendentals=cells, bytes_accessed=2 * drops * fields * nlat * nlon
         ),
-    )(entry_table, near_grid, cell_table)
+    )(entry_table, near_grid, cell_table).reshape(drops, 4, targets)
 
 
 def solution(mesh):

time: 90.7 us -> 89 us (0.981)
  waiting for transfers between devices: 8.79 us -> 5.54 us
  Pallas kernels: 18.2 us -> 19.3 us
    all_to_all x1, waiting for transfers between devices: 8.78 us -> 5.54 us  [per_device(): lax.all_to_all(outgoing.reshape(devices, capacity, record.shape[1]), ('ro...]
    pallas_call x0 -> x1, other arithmetic: none -> 1.56 us  [near_field(): pl.pallas_call(functools.partial(near_kernel, points), grid=(drops,), in_...]
    pallas_call x1, Pallas kernels: 18.2 us -> 19.3 us  [near_field(): pl.pallas_call(functools.partial(near_kernel, points), grid=(drops,), in_...]
    unnamed x57 -> x41, local copies, waits for them, and re-layouts: 2.09 us -> 1.57 us
  transfers between devices with their start and end apart: 3 -> 3, of which waited for: 1 -> 1; matrix products, arithmetic and copies ran while one was open for 29% -> 38% of each run, Pallas kernels for 20% -> 22%
where the time goes in v2:
time: 89 us; the launch traced here: 87.8 us
  local copies, waits for them, and re-layouts  24.3 us (27%)
  starting transfers between devices  21.2 us (24%)
  Pallas kernels  19.3 us (22%)
  matrix products  9.25 us (10%)
  other arithmetic  6.86 us (8%)
  waiting for transfers between devices  5.54 us (6%)
  between operations  1.3 us (1%)
    pallas_call x1, Pallas kernels, near_field(): pl.pallas_call(functools.partial(near_kernel, points), grid=(drops,), in_...  19.3 us
    all_to_all x1, starting transfers between devices, per_device(): lax.all_to_all(jnp.broadcast_to(own_points.reshape(1, -1), (devices, drop...  11.2 us
    all_to_all x1, starting transfers between devices, per_device(): lax.all_to_all(outgoing.reshape(devices, capacity, record.shape[1]), ('ro...  10.1 us
    all_to_all x1, waiting for transfers between devices, per_device(): lax.all_to_all(outgoing.reshape(devices, capacity, record.shape[1]), ('ro...  5.54 us
    another operation x2, local copies, waits for them, and re-layouts, legendre_synth(): parted = coeff.reshape(batch_size, degrees, 2, orders)  5.23 us
    transpose x1, local copies, waits for them, and re-layouts, legendre_synth(): return jnp.einsum('mjl,nlcm->njcm', legendre, parted, precision=SPECTRAL)  4.6 us
    dot_general x1, local copies, waits for them, and re-layouts, fourier_synth(): jnp.einsum('njw,wk->njk', partial_legendre.reshape(batch_size, nlat, two...  3.9 us
    dot_general x2, matrix products, legendre_synth(): return jnp.einsum('mjl,nlcm->njcm', legendre, parted, precision=SPECTRAL)  2.69 us
  transfers between devices with their start and end apart: 3, of which 1 were waited for; matrix products, arithmetic and copies ran while one was open for 38% of the time, Pallas kernels for 22%

profile of v2, /device:TPU:0, one launch (start us, length us, event | category | flops | bytes accessed | tf_op | source)
XLA Modules:
  0.0 87.8 jit_solution(13221645565323940943)
XLA Ops:
  0.7 0.8 fusion.51
  1.5 1.1 %slice.68 = f32[16,1,64,128]{3,2,1,0:T(8,128)S(1)} slice(f32[16,3,64,128]{3,2,1,0:T(8,128)} %param.14), slice={[0:16], [0:1], [0:64], [0:128]} | slice | bytes 1048576 | tf_op jit(solution)/shard_map/slice | solution.py:160
  2.5 0.2 mul.330
  2.7 2.2 %fusion = bf16[16,4]{0,1:T(4,128)(2,1)S(1)} fusion(f32[8192,4]{0,1:T(4,128)} %constant.118.clone, f32[2,8,64,128]{3,2,1,0:T(8,128)S(1)} %bitcast.140, f32[2,8,64,128]{3,2,1,0:T(8,128)S(1)} %bitcast.139, f32[8192]{0:T(1024)S(1)} %get-tuple-element.39), kind=kOutput, calls=%fused_computation.9 | convolution fusion | flops 3407936 | bytes 1212544 | tf_op jit(solution)/shard_map/dot_general | solution.py:194
  5.0 0.1 copy.132
  5.1 0.1 broadcast_in_dim.4
  5.2 0.7 broadcast_in_dim.5
  5.9 11.2 %all-to-all-start = ((bf16[128,1,64]{2,1,0:T(2,128)(2,1)}), bf16[128,1,64]{2,1,0:T(2,128)(2,1)S(1)}, u32[]{:S(2)}, u32[]{:S(2)}) async-start(bf16[128,1,64]{2,1,0:T(2,128)(2,1)} %broadcast_in_dim.5), calls=%async_computation | async-start | bytes 131072 | tf_op jit(solution)/shard_map/all_to_all | solution.py:232
  17.3 0.1 copy.173
  17.4 0.1 copy.174
  17.5 0.1 copy.172
  17.8 0.4 convolution_bitcast_fusion.3
  18.2 1.2 %fusion.61 = (bf16[16,64,128]{2,1,0:T(8,128)(2,1)}, f32[16,64,128]{2,1,0:T(8,128)}) fusion(bf16[2,64,128]{2,1,0:T(8,128)(2,1)S(1)} %copy-done.11, s32[]{:T(128)S(6)} %select_n.48, bf16[16,64,2,32]{1,0,2,3:T(8,128)(2,1)S(1)} %convolution_bitcast_fusion.3), kind=kOutput, calls=%fused_computation.115 | convolution fusion | flops 16908288 | bytes 1064964 | tf_op jit(solution)/shard_map/njw,wk->njk/dot_general | solution.py:134
  19.4 1.0 %broadcast_multiply_fusion = (bf16[16,1,64,128]{3,2,1,0:T(8,128)(2,1)S(1)}, bf16[16,1,64,128]{3,2,1,0:T(8,128)(2,1)S(1)}, bf16[16,1,64,128]{3,2,1,0:T(8,128)(2,1)S(1)}, bf16[16,1,64,128]{3,2,1,0:T(8,128)(2,1)S(1)}) fusion(f32[64]{0:T(128)S(1)} %get-tuple-element.42, f32[16,64]{1,0:T(8,128)S(1)} %fusion.51, f32[64,128]{1,0:T(8,128)S(1)} %get-tuple-element.38, ...), kind=kLoop, calls=%fused_computation.45 | loop fusion | flops 1572864 | bytes 2658816 | tf_op jit(solution)/shard_map/mul | solution.py:162
  20.4 0.1 pad_maximum_fusion
  20.6 0.8 reshape_reshape.6
  21.4 4.4 %copy.138 = bf16[64,64,2,64]{1,0,2,3:T(8,128)(2,1)} copy(bf16[64,64,2,64]{3,2,1,0:T(2,128)(2,1)S(1)} %reshape_reshape.6) | data formatting | bytes 2097152 | tf_op jit(solution)/shard_map/reshape;reshape | solution.py:128
  25.8 2.3 %convolution_bitcast_fusion = bf16[64,64,2,64]{1,0,2,3:T(8,128)(2,1)S(1)} fusion(bf16[64,64,2,64]{1,0,2,3:T(8,128)(2,1)} %copy.138, bf16[64,64,64,1]{2,1,3,0:T(8,128)(2,1)S(1)} %copy-done.1), kind=kOutput, calls=%fused_computation | convolution fusion | flops 67108864 | bytes 2621440 | tf_op jit(solution)/shard_map/mjl,nlcm->njcm/dot_general | solution.py:129
  28.1 4.6 %copy.139 = bf16[64,64,2,64]{3,2,1,0:T(2,128)(2,1)} copy(bf16[64,64,2,64]{1,0,2,3:T(8,128)(2,1)S(1)} %convolution_bitcast_fusion) | data formatting | bytes 2097152 | tf_op jit(solution)/shard_map/mjl,nlcm->njcm/transpose | solution.py:129
  32.7 3.9 %dot_general.41 = bf16[16,4,64,128]{3,2,1,0:T(8,128)(2,1)S(1)} reshape(bf16[64,64,2,64]{3,2,1,0:T(2,128)(2,1)} %copy.139) | data formatting | bytes 2097152 | tf_op jit(solution)/shard_map/njw,wk->njk/dot_general | solution.py:134
  36.7 0.4 fusion.62
  37.1 0.3 fusion.18
  37.4 0.2 fusion.11
  37.6 0.2 copy-done.9
  38.0 0.1 fusion.37
  38.1 0.2 reduce_window_sum.11
  38.2 0.2 select_reduce_fusion
  38.5 0.8 pad_maximum_fusion.1.g_ref
  39.6 0.1 add.129
  39.7 0.1 add.130
  39.8 0.1 add.131
  40.0 0.1 mul.338
  40.2 0.1 convert_element_type.71
  40.3 0.2 reduce.1
  40.5 0.6 reshape.241
  41.1 0.4 fusion.5
  41.4 0.1 copy.134
  41.6 0.1 reshape.242
  42.0 0.2 copy.137
  42.1 0.8 reshape.243.t_ref
  42.9 19.3 %shard_map.157 = f32[16,128,1]{2,1,0:T(8,128)} custom-call(f32[1408]{0:T(1024)} %reshape.243.t_ref, bf16[16,2,64,128]{3,2,1,0:T(8,128)(2,1)} %pad_maximum_fusion.1.g_ref, f32[8,64,128]{2,1,0:T(8,128)} %constant.119.clone.c_ref), custom_call_target="tpu_custom_call" | custom-call | flops 100663296 | bytes 524288 | tf_op jit(solution)/shard_map/pallas_call | solution.py:393
  62.2 1.6 %reduce.2 = f32[16,128]{1,0:T(8,128)S(1)} reduce(f32[16,128,1]{2,1,0:T(8,128)} %shard_map.157, f32[]{:T(128)} %constant.134), dimensions={2}, to_apply=%pallas_call.3.reduce_sub_computation | reduce | bytes 16388 | tf_op jit(solution)/shard_map/pallas_call | solution.py:393
  64.0 0.1 copy.158
  64.1 0.1 reshape.253
  64.2 1.0 %fusion.33 = f32[256,13]{1,0:T(8,128)} fusion(s32[128]{0:T(128)S(1)} %multiply_add_fusion.2, f32[128,1]{0,1:T(1,128)S(1)} %convert_element_type.71, f32[128,12]{0,1:T(8,128)S(1)} %reshape.253), kind=kOutput, calls=%fused_computation.64 | convolution fusion | flops 5179008 | bytes 20480 | tf_op jit(solution)/shard_map/dot_general | solution.py:284
  65.2 10.1 %all-to-all-start.1 = ((f32[128,2,13]{2,1,0:T(2,128)}), f32[128,2,13]{2,1,0:T(2,128)S(1)}, u32[]{:S(2)}, u32[]{:S(2)}) async-start(f32[128,2,13]{2,1,0:T(2,128)} %bitcast.35), calls=%async_computation.1 | async-start | bytes 262144 | tf_op jit(solution)/shard_map/all_to_all | solution.py:285
  75.3 0.2 convolution_multiply_fusion
  75.5 0.2 reshape.245
  75.8 0.7 copy.143
  76.5 0.4 convolution_bitcast_fusion.1
  76.9 0.7 copy.144
  77.6 0.6 reshape.246
  78.2 1.0 %multiply_multiply_fusion.5 = f32[16,64,128]{2,1,0:T(8,128)} fusion(f32[16,64,128]{2,1,0:T(8,128)S(1)} %reshape.246, f32[64,128]{1,0:T(8,128)S(1)} %get-tuple-element.38, f32[16,64]{1,0:T(8,128)S(1)} %fusion.51), kind=kLoop, calls=%fused_computation.43 | loop fusion | flops 262144 | bytes 1085440 | tf_op jit(solution)/shard_map/mul | solution.py:298
  79.2 5.5 %all-to-all-done.1 = f32[128,2,13]{2,1,0:T(2,128)S(1)} async-done(((f32[128,2,13]{2,1,0:T(2,128)}), f32[128,2,13]{2,1,0:T(2,128)S(1)}, u32[]{:S(2)}, u32[]{:S(2)}) %all-to-all-start.1) | async-done | bytes 13344 | tf_op jit(solution)/shard_map/all_to_all | solution.py:285
  84.7 0.2 slice_reduce_fusion
  84.9 0.3 fusion.26
  85.2 0.1 copy.162
  85.3 0.7 reshape.257
  86.0 0.2 convolution_multiply_fusion.1
  86.3 0.1 reshape.249
  86.4 0.2 constant_dynamic-slice_fusion
  86.6 0.1 copy.178
  86.7 0.3 convolution_bitcast_fusion.4
  87.1 0.8 copy.163
  (73 shorter events, 1.6 us)
Async XLA Ops:
  0.6 37.8 %copy-start = (f32[256,2]{0,1:T(2,128)S(1)}, f32[256,2]{0,1:T(2,128)}, u32[]{:S(2)}) copy-start(f32[256,2]{0,1:T(2,128)} %param.18) | copy-start | bytes 6148
  0.6 16.6 %copy-start.6 = (f32[4,3,64,64]{3,2,1,0:T(8,128)S(1)}, f32[4,3,64,64]{3,2,1,0:T(8,128)}, u32[]{:S(2)}) copy-start(f32[4,3,64,64]{3,2,1,0:T(8,128)} %param.17) | copy-start | bytes 589828
  2.7 15.1 %copy-start.4 = (bf16[64,64,64]{2,1,0:T(8,128)(2,1)S(1)}, bf16[64,64,64]{2,1,0:T(8,128)(2,1)}, u32[]{:S(2)}) copy-start(bf16[64,64,64]{2,1,0:T(8,128)(2,1)} %constant.207) | copy-start | bytes 1572868
  5.2 13.0 %copy-start.11 = (bf16[2,64,128]{2,1,0:T(8,128)(2,1)S(1)}, bf16[2,64,128]{2,1,0:T(8,128)(2,1)}, u32[]{:S(2)}) copy-start(bf16[2,64,128]{2,1,0:T(8,128)(2,1)} %constant.208) | copy-start | bytes 98308
  5.9 34.4 %all-to-all-start = ((bf16[128,1,64]{2,1,0:T(2,128)(2,1)}), bf16[128,1,64]{2,1,0:T(2,128)(2,1)S(1)}, u32[]{:S(2)}, u32[]{:S(2)}) async-start(bf16[128,1,64]{2,1,0:T(2,128)(2,1)} %broadcast_in_dim.5), calls=%async_computation | async-start | bytes 131072 | tf_op jit(solution)/shard_map/all_to_all | solution.py:232
  17.1 2.3 %copy-start.14 = (f32[64]{0:T(128)}, f32[64]{0:T(128)S(1)}, u32[]{:S(2)}) copy-start(f32[64]{0:T(128)S(1)} %get-tuple-element.43) | copy-start | bytes 772
  17.3 2.1 %copy-start.2 = (f32[16,3,64,128]{3,2,1,0:T(8,128)S(1)}, f32[16,3,64,128]{3,2,1,0:T(8,128)}, u32[]{:S(2)}) copy-start(f32[16,3,64,128]{3,2,1,0:T(8,128)} %param.14) | copy-start | bytes 4718596
  19.4 66.6 %collective-permute-start = (bf16[16,64,128]{2,1,0:T(8,128)(2,1)}, bf16[16,64,128]{2,1,0:T(8,128)(2,1)S(1)}, u32[]{:S(2)}, u32[]{:S(2)}) collective-permute-start(bf16[16,64,128]{2,1,0:T(8,128)(2,1)} %get-tuple-element.40), channel_id=1, source_target_pairs={{0,16},{16,0},{32,48},{48,32},{64,80},{80,64},{96,112},{112,96},{1... | collective-permute-start | bytes 786440 | tf_op jit(solution)/shard_map/ppermute | solution.py:24
  21.4 4.4 %copy-start.1 = (bf16[64,64,64,1]{2,1,3,0:T(8,128)(2,1)S(1)}, bf16[64,64,64,1]{2,1,3,0:T(8,128)(2,1)}, u32[]{:S(2)}) copy-start(bf16[64,64,64,1]{2,1,3,0:T(8,128)(2,1)} %constant.204) | copy-start | bytes 1572868
  32.7 3.9 %copy-start.15 = (f32[16,2]{0,1:T(2,128)S(1)}, f32[16,2]{0,1:T(2,128)}, u32[]{:S(2)}) copy-start(f32[16,2]{0,1:T(2,128)} %param.16) | copy-start | bytes 388
  32.7 3.9 %copy-start.7 = (bf16[128,128,1,1]{1,0,3,2:T(8,128)(2,1)S(1)}, bf16[128,128,1,1]{1,0,3,2:T(8,128)(2,1)}, u32[]{:S(2)}) copy-start(bf16[128,128,1,1]{1,0,3,2:T(8,128)(2,1)} %constant.205) | copy-start | bytes 98308
  37.1 0.7 copy-start.9
  37.1 0.8 copy-start.12
  37.4 2.1 %copy-start.10 = (f32[3,16,8]{1,2,0:T(8,128)S(1)}, f32[3,16,8]{1,2,0:T(8,128)}, u32[]{:S(2)}) copy-start(f32[3,16,8]{1,2,0:T(8,128)} %param.19) | copy-start | bytes 4612
  37.4 2.5 %copy-start.13 = (f32[3,4]{1,0:T(4,128)S(1)}, f32[3,4]{1,0:T(4,128)}, u32[]{:S(2)}) copy-start(f32[3,4]{1,0:T(4,128)} %constant.128) | copy-start | bytes 148
  42.9 32.4 %copy-start.8 = (bf16[128,128,1]{1,0,2:T(8,128)(2,1)S(1)}, bf16[128,128,1]{1,0,2:T(8,128)(2,1)}, u32[]{:S(2)}) copy-start(bf16[128,128,1]{1,0,2:T(8,128)(2,1)} %constant.206) | copy-start | bytes 98308
  42.9 32.4 %copy-start.16 = (f32[64]{0:T(128)S(1)}, f32[64]{0:T(128)}, u32[]{:S(2)}) copy-start(f32[64]{0:T(128)} %constant.116.clone) | copy-start | bytes 772
  65.2 19.5 %all-to-all-start.1 = ((f32[128,2,13]{2,1,0:T(2,128)}), f32[128,2,13]{2,1,0:T(2,128)S(1)}, u32[]{:S(2)}, u32[]{:S(2)}) async-start(f32[128,2,13]{2,1,0:T(2,128)} %bitcast.35), calls=%async_computation.1 | async-start | bytes 262144 | tf_op jit(solution)/shard_map/all_to_all | solution.py:285
  76.9 9.1 %copy-start.3 = (f32[16,64,128]{2,1,0:T(8,128)S(1)}, f32[16,64,128]{2,1,0:T(8,128)}, u32[]{:S(2)}) copy-start(f32[16,64,128]{2,1,0:T(8,128)} %get-tuple-element.41) | copy-start | bytes 1572868
  78.1 8.6 %copy-start.5 = (bf16[64,64,64]{2,1,0:T(8,128)(2,1)S(1)}, bf16[64,64,64]{2,1,0:T(8,128)(2,1)}, u32[]{:S(2)}) copy-start(bf16[64,64,64]{2,1,0:T(8,128)(2,1)} %constant.207) | copy-start | bytes 1572868

commit v3 on v1

--- a/solution.py
+++ b/solution.py
@@ -192,7 +192,9 @@
     prepared = prepare(coeffs, keep_mask)
     point_weight = point_table(degrees)
     point_surface = jnp.dot(
-        prepared[:, 0].reshape(drop_count, degrees * coef_width), point_weight, precision=HIGH
+        (coeffs[:, 0] * keep_mask).reshape(drop_count, degrees * coef_width),
+        point_weight,
+        precision=lax.Precision.HIGH,
     )
     own_points = jnp.exp(point_surface).astype(jnp.bfloat16)
     partial_legendre = legendre_synth(
@@ -258,9 +260,7 @@
     ).reshape(-1)
     cell_table = cell_tables(nlat, nlon, point_count)
     partial = near_field(entry_table, near_grid, cell_table, readers, point_count)
-    partial, traction_grid, split_grid = lax.optimization_barrier(
-        (partial, traction_grid, split_grid)
-    )
+    partial, traction_grid = lax.optimization_barrier((partial, traction_grid))
     sums = jnp.sum(partial, axis=3)
     contribution = (
         sums[:, :3] + jnp.transpose(target_point, (0, 2, 1)) * sums[:, 3:]

time: 90.7 us -> 87.8 us (0.968)
  waiting for transfers between devices: 8.79 us -> 5.54 us
    all_to_all x1, waiting for transfers between devices: 8.78 us -> 5.54 us  [per_device(): lax.all_to_all(outgoing.reshape(devices, capacity, record.shape[1]), ('ro...]
    reduce_sum x1, other arithmetic: 0.37 us -> 1.57 us  [per_device(): sums = jnp.sum(partial, axis=3)]
    slice x0 -> x1, local copies, waits for them, and re-layouts: none -> 1.08 us  [per_device(): coeffs[:, 0] * keep_mask]
    slice x2 -> x1, local copies, waits for them, and re-layouts: 1.11 us -> 0.03 us  [prepare(): shape_part = coeffs[:, 0] * keep_mask]
    unnamed x57 -> x41, local copies, waits for them, and re-layouts: 2.09 us -> 1.57 us
  transfers between devices with their start and end apart: 3 -> 3, of which waited for: 1 -> 1; matrix products, arithmetic and copies ran while one was open for 29% -> 38% of each run, Pallas kernels for 20% -> 21%
where the time goes in v3:
time: 87.8 us; the launch traced here: 86.6 us
  local copies, waits for them, and re-layouts  24.2 us (28%)
  starting transfers between devices  21.2 us (24%)
  Pallas kernels  18.1 us (21%)
  matrix products  9.25 us (11%)
  other arithmetic  6.87 us (8%)
  waiting for transfers between devices  5.54 us (6%)
  between operations  1.29 us (1%)
    pallas_call x1, Pallas kernels, near_field(): pl.pallas_call(functools.partial(near_kernel, points), grid=(drops,), in_...  18.1 us
    all_to_all x1, starting transfers between devices, per_device(): lax.all_to_all(jnp.broadcast_to(own_points.reshape(1, -1), (devices, drop...  11.2 us
    all_to_all x1, starting transfers between devices, per_device(): lax.all_to_all(outgoing.reshape(devices, capacity, record.shape[1]), ('ro...  10.1 us
    all_to_all x1, waiting for transfers between devices, per_device(): lax.all_to_all(outgoing.reshape(devices, capacity, record.shape[1]), ('ro...  5.54 us
    another operation x2, local copies, waits for them, and re-layouts, legendre_synth(): parted = coeff.reshape(batch_size, degrees, 2, orders)  5.23 us
    transpose x1, local copies, waits for them, and re-layouts, legendre_synth(): return jnp.einsum('mjl,nlcm->njcm', legendre, parted, precision=SPECTRAL)  4.6 us
    dot_general x1, local copies, waits for them, and re-layouts, fourier_synth(): jnp.einsum('njw,wk->njk', partial_legendre.reshape(batch_size, nlat, two...  3.9 us
    dot_general x2, matrix products, legendre_synth(): return jnp.einsum('mjl,nlcm->njcm', legendre, parted, precision=SPECTRAL)  2.69 us
  transfers between devices with their start and end apart: 3, of which 1 were waited for; matrix products, arithmetic and copies ran while one was open for 38% of the time, Pallas kernels for 21%

profile of v3, /device:TPU:0, one launch (start us, length us, event | category | flops | bytes accessed | tf_op | source)
XLA Modules:
  0.0 86.6 jit_solution(12945837381974832319)
XLA Ops:
  0.7 0.8 fusion.51
  1.5 1.1 %slice.69 = f32[16,1,64,128]{3,2,1,0:T(8,128)S(1)} slice(f32[16,3,64,128]{3,2,1,0:T(8,128)} %param.14), slice={[0:16], [0:1], [0:64], [0:128]} | slice | bytes 1048576 | tf_op jit(solution)/shard_map/slice | solution.py:195
  2.5 0.2 mul.331
  2.7 2.2 %fusion = bf16[16,4]{0,1:T(4,128)(2,1)S(1)} fusion(f32[8192,4]{0,1:T(4,128)} %constant.118.clone, f32[2,8,64,128]{3,2,1,0:T(8,128)S(1)} %bitcast.141, f32[2,8,64,128]{3,2,1,0:T(8,128)S(1)} %bitcast.140, f32[8192]{0:T(1024)S(1)} %get-tuple-element.42), kind=kOutput, calls=%fused_computation.9 | convolution fusion | flops 3407936 | bytes 1212544 | tf_op jit(solution)/shard_map/dot_general | solution.py:194
  5.0 0.1 copy.168
  5.1 0.1 broadcast_in_dim.4
  5.2 0.7 broadcast_in_dim.5
  5.9 11.2 %all-to-all-start = ((bf16[128,1,64]{2,1,0:T(2,128)(2,1)}), bf16[128,1,64]{2,1,0:T(2,128)(2,1)S(1)}, u32[]{:S(2)}, u32[]{:S(2)}) async-start(bf16[128,1,64]{2,1,0:T(2,128)(2,1)} %broadcast_in_dim.5), calls=%async_computation | async-start | bytes 131072 | tf_op jit(solution)/shard_map/all_to_all | solution.py:232
  17.3 0.1 copy.209
  17.4 0.1 copy.210
  17.5 0.1 copy.208
  17.8 0.4 convolution_bitcast_fusion.3
  18.2 1.2 %fusion.61 = (bf16[16,64,128]{2,1,0:T(8,128)(2,1)}, f32[16,64,128]{2,1,0:T(8,128)}) fusion(bf16[2,64,128]{2,1,0:T(8,128)(2,1)S(1)} %copy-done.11, s32[]{:T(128)S(6)} %select_n.48, bf16[16,64,2,32]{1,0,2,3:T(8,128)(2,1)S(1)} %convolution_bitcast_fusion.3), kind=kOutput, calls=%fused_computation.115 | convolution fusion | flops 16908288 | bytes 1064964 | tf_op jit(solution)/shard_map/njw,wk->njk/dot_general | solution.py:134
  19.4 1.0 %broadcast_multiply_fusion = (bf16[16,1,64,128]{3,2,1,0:T(8,128)(2,1)S(1)}, bf16[16,1,64,128]{3,2,1,0:T(8,128)(2,1)S(1)}, bf16[16,1,64,128]{3,2,1,0:T(8,128)(2,1)S(1)}, bf16[16,1,64,128]{3,2,1,0:T(8,128)(2,1)S(1)}) fusion(f32[64]{0:T(128)S(1)} %get-tuple-element.45, f32[16,64]{1,0:T(8,128)S(1)} %fusion.51, f32[64,128]{1,0:T(8,128)S(1)} %get-tuple-element.41, ...), kind=kLoop, calls=%fused_computation.45 | loop fusion | flops 1572864 | bytes 2658816 | tf_op jit(solution)/shard_map/mul | solution.py:162
  20.4 0.1 pad_maximum_fusion
  20.6 0.8 reshape_reshape.6
  21.4 4.4 %copy.174 = bf16[64,64,2,64]{1,0,2,3:T(8,128)(2,1)} copy(bf16[64,64,2,64]{3,2,1,0:T(2,128)(2,1)S(1)} %reshape_reshape.6) | data formatting | bytes 2097152 | tf_op jit(solution)/shard_map/reshape;reshape | solution.py:128
  25.8 2.3 %convolution_bitcast_fusion = bf16[64,64,2,64]{1,0,2,3:T(8,128)(2,1)S(1)} fusion(bf16[64,64,2,64]{1,0,2,3:T(8,128)(2,1)} %copy.174, bf16[64,64,64,1]{2,1,3,0:T(8,128)(2,1)S(1)} %copy-done.1), kind=kOutput, calls=%fused_computation | convolution fusion | flops 67108864 | bytes 2621440 | tf_op jit(solution)/shard_map/mjl,nlcm->njcm/dot_general | solution.py:129
  28.1 4.6 %copy.175 = bf16[64,64,2,64]{3,2,1,0:T(2,128)(2,1)} copy(bf16[64,64,2,64]{1,0,2,3:T(8,128)(2,1)S(1)} %convolution_bitcast_fusion) | data formatting | bytes 2097152 | tf_op jit(solution)/shard_map/mjl,nlcm->njcm/transpose | solution.py:129
  32.7 3.9 %dot_general.41 = bf16[16,4,64,128]{3,2,1,0:T(8,128)(2,1)S(1)} reshape(bf16[64,64,2,64]{3,2,1,0:T(2,128)(2,1)} %copy.175) | data formatting | bytes 2097152 | tf_op jit(solution)/shard_map/njw,wk->njk/dot_general | solution.py:134
  36.7 0.4 fusion.62
  37.1 0.3 fusion.18
  37.4 0.2 fusion.11
  37.6 0.2 copy-done.9
  38.0 0.1 fusion.37
  38.1 0.2 reduce_window_sum.11
  38.2 0.2 select_reduce_fusion
  38.5 0.8 pad_maximum_fusion.1.g_ref
  39.6 0.1 add.129
  39.7 0.1 add.130
  39.8 0.1 add.131
  40.0 0.1 mul.339
  40.2 0.1 convert_element_type.71
  40.3 0.2 reduce.1
  40.5 0.6 reshape.239
  41.1 0.4 fusion.5
  41.4 0.1 copy.170
  41.6 0.1 reshape.240
  42.0 0.2 copy.173
  42.1 0.8 reshape.241.t_ref
  42.9 18.1 %shard_map.157 = f32[16,4,32,128]{3,2,1,0:T(8,128)} custom-call(f32[1408]{0:T(1024)} %reshape.241.t_ref, bf16[16,2,64,128]{3,2,1,0:T(8,128)(2,1)} %pad_maximum_fusion.1.g_ref, f32[8,64,128]{2,1,0:T(8,128)} %constant.119.clone.c_ref), custom_call_target="tpu_custom_call" | custom-call | flops 100663296 | bytes 524288 | tf_op jit(solution)/shard_map/pallas_call | solution.py:391
  61.1 1.6 %reduce_sum.29 = f32[16,4,32]{2,1,0:T(4,128)S(1)} reduce(f32[16,4,32,128]{3,2,1,0:T(8,128)} %shard_map.157, f32[]{:T(128)} %constant.95.clone.1), dimensions={3}, to_apply=%region_3.4 | reduce | flops 260096 | bytes 1056772 | tf_op jit(solution)/shard_map/reduce_sum | solution.py:264
  62.8 0.1 copy.194
  62.9 0.1 reshape.250
  63.0 1.0 %fusion.33 = f32[256,13]{1,0:T(8,128)} fusion(s32[128]{0:T(128)S(1)} %multiply_add_fusion.2, f32[128,1]{0,1:T(1,128)S(1)} %convert_element_type.71, f32[128,12]{0,1:T(8,128)S(1)} %reshape.250), kind=kOutput, calls=%fused_computation.64 | convolution fusion | flops 5179008 | bytes 20480 | tf_op jit(solution)/shard_map/dot_general | solution.py:284
  64.0 10.1 %all-to-all-start.1 = ((f32[128,2,13]{2,1,0:T(2,128)}), f32[128,2,13]{2,1,0:T(2,128)S(1)}, u32[]{:S(2)}, u32[]{:S(2)}) async-start(f32[128,2,13]{2,1,0:T(2,128)} %bitcast.35), calls=%async_computation.1 | async-start | bytes 262144 | tf_op jit(solution)/shard_map/all_to_all | solution.py:285
  74.1 0.2 convolution_multiply_fusion
  74.3 0.2 reshape.242
  74.6 0.7 copy.179
  75.3 0.4 convolution_bitcast_fusion.1
  75.6 0.7 copy.180
  76.3 0.6 reshape.243
  76.9 1.0 %multiply_multiply_fusion.5 = f32[16,64,128]{2,1,0:T(8,128)} fusion(f32[16,64,128]{2,1,0:T(8,128)S(1)} %reshape.243, f32[64,128]{1,0:T(8,128)S(1)} %get-tuple-element.41, f32[16,64]{1,0:T(8,128)S(1)} %fusion.51), kind=kLoop, calls=%fused_computation.43 | loop fusion | flops 262144 | bytes 1085440 | tf_op jit(solution)/shard_map/mul | solution.py:298
  77.9 5.5 %all-to-all-done.1 = f32[128,2,13]{2,1,0:T(2,128)S(1)} async-done(((f32[128,2,13]{2,1,0:T(2,128)}), f32[128,2,13]{2,1,0:T(2,128)S(1)}, u32[]{:S(2)}, u32[]{:S(2)}) %all-to-all-start.1) | async-done | bytes 13344 | tf_op jit(solution)/shard_map/all_to_all | solution.py:285
  83.4 0.2 slice_reduce_fusion
  83.6 0.3 fusion.26
  83.9 0.1 copy.198
  84.0 0.7 reshape.254
  84.8 0.2 convolution_multiply_fusion.1
  85.0 0.1 reshape.246
  85.1 0.2 constant_dynamic-slice_fusion
  85.4 0.1 copy.214
  85.5 0.3 convolution_bitcast_fusion.4
  85.8 0.8 copy.199
  (71 shorter events, 1.5 us)
Async XLA Ops:
  0.6 37.8 %copy-start = (f32[256,2]{0,1:T(2,128)S(1)}, f32[256,2]{0,1:T(2,128)}, u32[]{:S(2)}) copy-start(f32[256,2]{0,1:T(2,128)} %param.18) | copy-start | bytes 6148
  0.6 16.6 %copy-start.6 = (f32[4,3,64,64]{3,2,1,0:T(8,128)S(1)}, f32[4,3,64,64]{3,2,1,0:T(8,128)}, u32[]{:S(2)}) copy-start(f32[4,3,64,64]{3,2,1,0:T(8,128)} %param.17) | copy-start | bytes 589828
  2.7 15.1 %copy-start.4 = (bf16[64,64,64]{2,1,0:T(8,128)(2,1)S(1)}, bf16[64,64,64]{2,1,0:T(8,128)(2,1)}, u32[]{:S(2)}) copy-start(bf16[64,64,64]{2,1,0:T(8,128)(2,1)} %constant.206) | copy-start | bytes 1572868
  5.2 13.0 %copy-start.11 = (bf16[2,64,128]{2,1,0:T(8,128)(2,1)S(1)}, bf16[2,64,128]{2,1,0:T(8,128)(2,1)}, u32[]{:S(2)}) copy-start(bf16[2,64,128]{2,1,0:T(8,128)(2,1)} %constant.207) | copy-start | bytes 98308
  5.9 34.4 %all-to-all-start = ((bf16[128,1,64]{2,1,0:T(2,128)(2,1)}), bf16[128,1,64]{2,1,0:T(2,128)(2,1)S(1)}, u32[]{:S(2)}, u32[]{:S(2)}) async-start(bf16[128,1,64]{2,1,0:T(2,128)(2,1)} %broadcast_in_dim.5), calls=%async_computation | async-start | bytes 131072 | tf_op jit(solution)/shard_map/all_to_all | solution.py:232
  17.1 2.3 %copy-start.14 = (f32[64]{0:T(128)}, f32[64]{0:T(128)S(1)}, u32[]{:S(2)}) copy-start(f32[64]{0:T(128)S(1)} %get-tuple-element.46) | copy-start | bytes 772
  17.3 2.1 %copy-start.2 = (f32[16,3,64,128]{3,2,1,0:T(8,128)S(1)}, f32[16,3,64,128]{3,2,1,0:T(8,128)}, u32[]{:S(2)}) copy-start(f32[16,3,64,128]{3,2,1,0:T(8,128)} %param.14) | copy-start | bytes 4718596
  19.4 65.3 %collective-permute-start = (bf16[16,64,128]{2,1,0:T(8,128)(2,1)}, bf16[16,64,128]{2,1,0:T(8,128)(2,1)S(1)}, u32[]{:S(2)}, u32[]{:S(2)}) collective-permute-start(bf16[16,64,128]{2,1,0:T(8,128)(2,1)} %get-tuple-element.43), channel_id=1, source_target_pairs={{0,16},{16,0},{32,48},{48,32},{64,80},{80,64},{96,112},{112,96},{1... | collective-permute-start | bytes 786440 | tf_op jit(solution)/shard_map/ppermute | solution.py:24
  21.4 4.4 %copy-start.1 = (bf16[64,64,64,1]{2,1,3,0:T(8,128)(2,1)S(1)}, bf16[64,64,64,1]{2,1,3,0:T(8,128)(2,1)}, u32[]{:S(2)}) copy-start(bf16[64,64,64,1]{2,1,3,0:T(8,128)(2,1)} %constant.203) | copy-start | bytes 1572868
  32.7 3.9 %copy-start.15 = (f32[16,2]{0,1:T(2,128)S(1)}, f32[16,2]{0,1:T(2,128)}, u32[]{:S(2)}) copy-start(f32[16,2]{0,1:T(2,128)} %param.16) | copy-start | bytes 388
  32.7 3.9 %copy-start.7 = (bf16[128,128,1,1]{1,0,3,2:T(8,128)(2,1)S(1)}, bf16[128,128,1,1]{1,0,3,2:T(8,128)(2,1)}, u32[]{:S(2)}) copy-start(bf16[128,128,1,1]{1,0,3,2:T(8,128)(2,1)} %constant.204) | copy-start | bytes 98308
  37.1 0.7 copy-start.9
  37.1 0.8 copy-start.12
  37.4 2.1 %copy-start.10 = (f32[3,16,8]{1,2,0:T(8,128)S(1)}, f32[3,16,8]{1,2,0:T(8,128)}, u32[]{:S(2)}) copy-start(f32[3,16,8]{1,2,0:T(8,128)} %param.19) | copy-start | bytes 4612
  37.4 2.5 %copy-start.13 = (f32[3,4]{1,0:T(4,128)S(1)}, f32[3,4]{1,0:T(4,128)}, u32[]{:S(2)}) copy-start(f32[3,4]{1,0:T(4,128)} %constant.128) | copy-start | bytes 148
  42.9 31.1 %copy-start.8 = (bf16[128,128,1]{1,0,2:T(8,128)(2,1)S(1)}, bf16[128,128,1]{1,0,2:T(8,128)(2,1)}, u32[]{:S(2)}) copy-start(bf16[128,128,1]{1,0,2:T(8,128)(2,1)} %constant.205) | copy-start | bytes 98308
  42.9 31.1 %copy-start.16 = (f32[64]{0:T(128)S(1)}, f32[64]{0:T(128)}, u32[]{:S(2)}) copy-start(f32[64]{0:T(128)} %constant.116.clone) | copy-start | bytes 772
  64.0 19.5 %all-to-all-start.1 = ((f32[128,2,13]{2,1,0:T(2,128)}), f32[128,2,13]{2,1,0:T(2,128)S(1)}, u32[]{:S(2)}, u32[]{:S(2)}) async-start(f32[128,2,13]{2,1,0:T(2,128)} %bitcast.35), calls=%async_computation.1 | async-start | bytes 262144 | tf_op jit(solution)/shard_map/all_to_all | solution.py:285
  75.6 9.1 %copy-start.3 = (f32[16,64,128]{2,1,0:T(8,128)S(1)}, f32[16,64,128]{2,1,0:T(8,128)}, u32[]{:S(2)}) copy-start(f32[16,64,128]{2,1,0:T(8,128)} %get-tuple-element.44) | copy-start | bytes 1572868
  76.9 8.6 %copy-start.5 = (bf16[64,64,64]{2,1,0:T(8,128)(2,1)S(1)}, bf16[64,64,64]{2,1,0:T(8,128)(2,1)}, u32[]{:S(2)}) copy-start(bf16[64,64,64]{2,1,0:T(8,128)(2,1)} %constant.206) | copy-start | bytes 1572868

commit v4 on v3

--- a/solution.py
+++ b/solution.py
@@ -197,10 +197,15 @@
         precision=lax.Precision.HIGH,
     )
     own_points = jnp.exp(point_surface).astype(jnp.bfloat16)
-    partial_legendre = legendre_synth(
-        prepared.reshape(drop_count * 4, degrees, coef_width), legendre
-    )
-    surface = fourier_synth(partial_legendre, fourier).reshape(drop_count, 4, nlat, nlon)
+    batched = jnp.einsum(
+        "mjl,nlcm->mcnj",
+        legendre,
+        prepared.reshape(drop_count * 4, degrees, 2, degrees),
+        precision=SPECTRAL,
+    )
+    surface = jnp.einsum(
+        "mcnj,cmk->njk", batched, fourier.reshape(2, degrees, nlon), precision=SPECTRAL
+    ).reshape(drop_count, 4, nlat, nlon)
     radius, traction_grid = traction(surface, material)
     split_count = split_coeffs.shape[0]
     half_width = split_coeffs.shape[3]

time: 87.8 us -> 82 us (0.934)
  local copies, waits for them, and re-layouts: 24.2 us -> 18 us
    reshape x0 -> x2, local copies, waits for them, and re-layouts: none -> 7.52 us  [per_device(): prepared.reshape(drop_count * 4, degrees, 2, degrees)]
    another operation x2 -> x0, local copies, waits for them, and re-layouts: 5.23 us -> none  [legendre_synth(): parted = coeff.reshape(batch_size, degrees, 2, orders)]
    transpose x1 -> x0, local copies, waits for them, and re-layouts: 4.6 us -> none  [legendre_synth(): return jnp.einsum('mjl,nlcm->njcm', legendre, parted, precision=SPECTRAL)]
    dot_general x1 -> x0, local copies, waits for them, and re-layouts: 3.9 us -> none  [fourier_synth(): jnp.einsum('njw,wk->njk', partial_legendre.reshape(batch_size, nlat, two...]
    dot_general x0 -> x2, matrix products: none -> 3.04 us  [the longest x1 2.34 us: per_device(): jnp.einsum('mcnj,cmk->njk', batched, fourier.reshape(2, degrees, nlon), p...]
    dot_general x2 -> x1, matrix products: 2.69 us -> 0.39 us  [legendre_synth(): return jnp.einsum('mjl,nlcm->njcm', legendre, parted, precision=SPECTRAL)]
  transfers between devices with their start and end apart: 3 -> 3, of which waited for: 1 -> 1; matrix products, arithmetic and copies ran while one was open for 38% -> 34% of each run, Pallas kernels for 21% -> 22%
where the time goes in v4:
time: 82 us; the launch traced here: 80.7 us
  starting transfers between devices  21.2 us (26%)
  Pallas kernels  18.1 us (22%)
  local copies, waits for them, and re-layouts  18 us (22%)
  matrix products  9.58 us (12%)
  other arithmetic  6.87 us (8%)
  waiting for transfers between devices  5.55 us (7%)
  between operations  1.28 us (2%)
    pallas_call x1, Pallas kernels, near_field(): pl.pallas_call(functools.partial(near_kernel, points), grid=(drops,), in_...  18.1 us
    all_to_all x1, starting transfers between devices, per_device(): lax.all_to_all(jnp.broadcast_to(own_points.reshape(1, -1), (devices, drop...  11.2 us
    all_to_all x1, starting transfers between devices, per_device(): lax.all_to_all(outgoing.reshape(devices, capacity, record.shape[1]), ('ro...  10.1 us
    reshape x2, local copies, waits for them, and re-layouts, per_device(): prepared.reshape(drop_count * 4, degrees, 2, degrees)  7.52 us
    all_to_all x1, waiting for transfers between devices, per_device(): lax.all_to_all(outgoing.reshape(devices, capacity, record.shape[1]), ('ro...  5.54 us
    dot_general x1, matrix products, per_device(): jnp.einsum('mcnj,cmk->njk', batched, fourier.reshape(2, degrees, nlon), p...  2.34 us
    dot_general x1, matrix products, per_device(): jnp.dot((coeffs[:, 0] * keep_mask).reshape(drop_count, degrees * coef_wid...  2.22 us
  transfers between devices with their start and end apart: 3, of which 1 were waited for; matrix products, arithmetic and copies ran while one was open for 34% of the time, Pallas kernels for 22%

profile of v4, /device:TPU:0, one launch (start us, length us, event | category | flops | bytes accessed | tf_op | source)
XLA Modules:
  0.0 80.7 jit_solution(4566924102026276207)
XLA Ops:
  0.7 0.8 fusion.56
  1.5 1.1 %slice.69 = f32[16,1,64,128]{3,2,1,0:T(8,128)S(1)} slice(f32[16,3,64,128]{3,2,1,0:T(8,128)} %param.14), slice={[0:16], [0:1], [0:64], [0:128]} | slice | bytes 1048576 | tf_op jit(solution)/shard_map/slice | solution.py:195
  2.5 0.2 mul.331
  2.7 2.2 %fusion.5 = bf16[16,4]{0,1:T(4,128)(2,1)S(1)} fusion(f32[8192,4]{0,1:T(4,128)} %constant.118.clone, f32[2,8,64,128]{3,2,1,0:T(8,128)S(1)} %bitcast.145, f32[2,8,64,128]{3,2,1,0:T(8,128)S(1)} %bitcast.144, f32[8192]{0:T(1024)S(1)} %get-tuple-element.42), kind=kOutput, calls=%fused_computation.11 | convolution fusion | flops 3407936 | bytes 1212544 | tf_op jit(solution)/shard_map/dot_general | solution.py:194
  5.0 0.1 copy.169
  5.1 0.1 broadcast_in_dim.4
  5.2 0.7 broadcast_in_dim.5
  5.9 11.2 %all-to-all-start = ((bf16[128,1,64]{2,1,0:T(2,128)(2,1)}), bf16[128,1,64]{2,1,0:T(2,128)(2,1)S(1)}, u32[]{:S(2)}, u32[]{:S(2)}) async-start(bf16[128,1,64]{2,1,0:T(2,128)(2,1)} %broadcast_in_dim.5), calls=%async_computation | async-start | bytes 131072 | tf_op jit(solution)/shard_map/all_to_all | solution.py:237
  17.3 0.1 copy.211
  17.4 0.1 copy.212
  17.5 0.1 copy.210
  17.8 0.4 convolution_bitcast_fusion.2
  18.2 1.2 %fusion.66 = (bf16[16,64,128]{2,1,0:T(8,128)(2,1)}, f32[16,64,128]{2,1,0:T(8,128)}) fusion(bf16[2,64,128]{2,1,0:T(8,128)(2,1)S(1)} %copy-done.11, s32[]{:T(128)S(6)} %select_n.48, bf16[16,64,2,32]{1,0,2,3:T(8,128)(2,1)S(1)} %convolution_bitcast_fusion.2), kind=kOutput, calls=%fused_computation.117 | convolution fusion | flops 16908288 | bytes 1064964 | tf_op jit(solution)/shard_map/njw,wk->njk/dot_general | solution.py:134
  19.4 1.0 %broadcast_multiply_fusion = (bf16[16,1,64,128]{3,2,1,0:T(8,128)(2,1)S(1)}, bf16[16,1,64,128]{3,2,1,0:T(8,128)(2,1)S(1)}, bf16[16,1,64,128]{3,2,1,0:T(8,128)(2,1)S(1)}, bf16[16,1,64,128]{3,2,1,0:T(8,128)(2,1)S(1)}) fusion(f32[64]{0:T(128)S(1)} %get-tuple-element.45, f32[16,64]{1,0:T(8,128)S(1)} %fusion.56, f32[64,128]{1,0:T(8,128)S(1)} %get-tuple-element.41, ...), kind=kLoop, calls=%fused_computation.47 | loop fusion | flops 1572864 | bytes 2658816 | tf_op jit(solution)/shard_map/mul | solution.py:162
  20.4 0.1 pad_maximum_fusion
  20.6 1.9 %reshape.244 = bf16[64,64,2,64]{3,2,1,0:T(2,128)(2,1)} reshape(bf16[16,4,64,128]{3,2,1,0:T(8,128)(2,1)S(1)} %pad_maximum_fusion) | data formatting | bytes 2097152 | tf_op jit(solution)/shard_map/reshape | solution.py:203
  22.4 5.7 %copy.175 = bf16[64,64,2,64]{1,0,2,3:T(8,128)(2,1)S(1)} copy(bf16[64,64,2,64]{3,2,1,0:T(2,128)(2,1)} %reshape.244) | data formatting | bytes 2097152 | tf_op jit(solution)/shard_map/reshape | solution.py:203
  28.2 0.7 fusion.67
  28.9 2.3 %fusion.2 = f32[16,4,64,128]{3,2,1,0:T(8,128)S(1)} fusion(bf16[2,64,128,1,1]{2,1,0,4,3:T(8,128)(2,1)S(1)} %copy-done.7, bf16[16,4,64,2,64]{2,1,0,3,4:T(4,128)(2,1)S(1)} %bitcast.143), kind=kOutput, calls=%fused_computation.3 | convolution fusion | flops 134217728 | bytes 3178496 | tf_op jit(solution)/shard_map/mcnj,cmk->njk/dot_general | solution.py:206
  31.3 0.3 fusion.23
  31.6 0.2 fusion.16
  31.8 0.2 copy-done.9
  32.0 0.1 reshape.251
  32.1 0.1 fusion.42
  32.2 0.2 reduce_window_sum.11
  32.4 0.2 select_reduce_fusion
  32.7 0.8 %pad_maximum_fusion.1.g_ref = bf16[16,2,64,128]{3,2,1,0:T(8,128)(2,1)} fusion(bf16[16,1,64,128]{3,2,1,0:T(8,128)(2,1)S(1)} %get-tuple-element.27, bf16[16,1,64,128]{3,2,1,0:T(8,128)(2,1)S(1)} %get-tuple-element.26), kind=kLoop, calls=%fused_computation.37 | loop fusion | flops 262144 | bytes 1048576 | tf_op jit(solution)/shard_map/stack | solution.py:233
  33.6 0.1 eq.62
  33.8 0.1 add.129
  33.9 0.1 add.130
  34.0 0.1 add.131
  34.1 0.1 mul.339
  34.3 0.1 convert_element_type.71
  34.4 0.2 reduce.1
  34.6 0.6 reshape.241
  35.2 0.4 fusion.10
  35.6 0.1 copy.171
  35.7 0.1 reshape.242
  36.1 0.2 copy.174
  36.3 0.8 reshape.243.t_ref
  37.1 18.1 %shard_map.157 = f32[16,4,32,128]{3,2,1,0:T(8,128)} custom-call(f32[1408]{0:T(1024)} %reshape.243.t_ref, bf16[16,2,64,128]{3,2,1,0:T(8,128)(2,1)} %pad_maximum_fusion.1.g_ref, f32[8,64,128]{2,1,0:T(8,128)} %constant.119.clone.c_ref), custom_call_target="tpu_custom_call" | custom-call | flops 100663296 | bytes 524288 | tf_op jit(solution)/shard_map/pallas_call | solution.py:396
  55.2 1.6 %reduce_sum.29 = f32[16,4,32]{2,1,0:T(4,128)S(1)} reduce(f32[16,4,32,128]{3,2,1,0:T(8,128)} %shard_map.157, f32[]{:T(128)} %constant.95.clone.1), dimensions={3}, to_apply=%region_3.4 | reduce | flops 260096 | bytes 1056772 | tf_op jit(solution)/shard_map/reduce_sum | solution.py:269
  56.9 0.1 copy.195
  57.0 0.1 reshape.253
  57.1 1.0 %fusion.38 = f32[256,13]{1,0:T(8,128)} fusion(s32[128]{0:T(128)S(1)} %multiply_add_fusion.2, f32[128,1]{0,1:T(1,128)S(1)} %convert_element_type.71, f32[128,12]{0,1:T(8,128)S(1)} %reshape.253), kind=kOutput, calls=%fused_computation.66 | convolution fusion | flops 5179008 | bytes 20480 | tf_op jit(solution)/shard_map/dot_general | solution.py:289
  58.1 10.1 %all-to-all-start.1 = ((f32[128,2,13]{2,1,0:T(2,128)}), f32[128,2,13]{2,1,0:T(2,128)S(1)}, u32[]{:S(2)}, u32[]{:S(2)}) async-start(f32[128,2,13]{2,1,0:T(2,128)} %bitcast.38), calls=%async_computation.1 | async-start | bytes 262144 | tf_op jit(solution)/shard_map/all_to_all | solution.py:290
  68.2 0.2 convolution_multiply_fusion
  68.4 0.2 reshape.246
  68.7 0.7 copy.180
  69.4 0.4 convolution_bitcast_fusion
  69.8 0.7 copy.181
  70.4 0.6 reshape.247
  71.0 1.0 %multiply_multiply_fusion.5 = f32[16,64,128]{2,1,0:T(8,128)} fusion(f32[16,64,128]{2,1,0:T(8,128)S(1)} %reshape.247, f32[64,128]{1,0:T(8,128)S(1)} %get-tuple-element.41, f32[16,64]{1,0:T(8,128)S(1)} %fusion.56), kind=kLoop, calls=%fused_computation.45 | loop fusion | flops 262144 | bytes 1085440 | tf_op jit(solution)/shard_map/mul | solution.py:303
  72.0 5.5 %all-to-all-done.1 = f32[128,2,13]{2,1,0:T(2,128)S(1)} async-done(((f32[128,2,13]{2,1,0:T(2,128)}), f32[128,2,13]{2,1,0:T(2,128)S(1)}, u32[]{:S(2)}, u32[]{:S(2)}) %all-to-all-start.1) | async-done | bytes 13344 | tf_op jit(solution)/shard_map/all_to_all | solution.py:290
  77.6 0.2 slice_reduce_fusion
  77.8 0.3 fusion.31
  78.1 0.1 copy.199
  78.2 0.7 reshape.257
  78.9 0.2 convolution_multiply_fusion.1
  79.2 0.1 reshape.249
  79.3 0.2 constant_dynamic-slice_fusion
  79.5 0.1 copy.216
  79.6 0.3 convolution_bitcast_fusion.3
  79.9 0.8 copy.200
  (69 shorter events, 1.4 us)
Async XLA Ops:
  0.6 32.0 %copy-start = (f32[256,2]{0,1:T(2,128)S(1)}, f32[256,2]{0,1:T(2,128)}, u32[]{:S(2)}) copy-start(f32[256,2]{0,1:T(2,128)} %param.18) | copy-start | bytes 6148
  0.6 16.6 %copy-start.6 = (f32[4,3,64,64]{3,2,1,0:T(8,128)S(1)}, f32[4,3,64,64]{3,2,1,0:T(8,128)}, u32[]{:S(2)}) copy-start(f32[4,3,64,64]{3,2,1,0:T(8,128)} %param.17) | copy-start | bytes 589828
  2.7 15.1 %copy-start.4 = (bf16[64,64,64]{2,1,0:T(8,128)(2,1)S(1)}, bf16[64,64,64]{2,1,0:T(8,128)(2,1)}, u32[]{:S(2)}) copy-start(bf16[64,64,64]{2,1,0:T(8,128)(2,1)} %constant.207) | copy-start | bytes 1572868
  5.2 13.0 %copy-start.11 = (bf16[2,64,128]{2,1,0:T(8,128)(2,1)S(1)}, bf16[2,64,128]{2,1,0:T(8,128)(2,1)}, u32[]{:S(2)}) copy-start(bf16[2,64,128]{2,1,0:T(8,128)(2,1)} %constant.208) | copy-start | bytes 98308
  5.9 28.5 %all-to-all-start = ((bf16[128,1,64]{2,1,0:T(2,128)(2,1)}), bf16[128,1,64]{2,1,0:T(2,128)(2,1)S(1)}, u32[]{:S(2)}, u32[]{:S(2)}) async-start(bf16[128,1,64]{2,1,0:T(2,128)(2,1)} %broadcast_in_dim.5), calls=%async_computation | async-start | bytes 131072 | tf_op jit(solution)/shard_map/all_to_all | solution.py:237
  17.1 2.3 %copy-start.14 = (f32[64]{0:T(128)}, f32[64]{0:T(128)S(1)}, u32[]{:S(2)}) copy-start(f32[64]{0:T(128)S(1)} %get-tuple-element.46) | copy-start | bytes 772
  17.3 2.1 %copy-start.2 = (f32[16,3,64,128]{3,2,1,0:T(8,128)S(1)}, f32[16,3,64,128]{3,2,1,0:T(8,128)}, u32[]{:S(2)}) copy-start(f32[16,3,64,128]{3,2,1,0:T(8,128)} %param.14) | copy-start | bytes 4718596
  19.4 59.5 %collective-permute-start = (bf16[16,64,128]{2,1,0:T(8,128)(2,1)}, bf16[16,64,128]{2,1,0:T(8,128)(2,1)S(1)}, u32[]{:S(2)}, u32[]{:S(2)}) collective-permute-start(bf16[16,64,128]{2,1,0:T(8,128)(2,1)} %get-tuple-element.43), channel_id=1, source_target_pairs={{0,16},{16,0},{32,48},{48,32},{64,80},{80,64},{96,112},{112,96},{1... | collective-permute-start | bytes 786440 | tf_op jit(solution)/shard_map/ppermute | solution.py:24
  22.4 5.7 %copy-start.15 = (f32[16,2]{0,1:T(2,128)S(1)}, f32[16,2]{0,1:T(2,128)}, u32[]{:S(2)}) copy-start(f32[16,2]{0,1:T(2,128)} %param.16) | copy-start | bytes 388
  22.4 5.7 %copy-start.1 = (bf16[64,64,64,1]{2,1,3,0:T(8,128)(2,1)S(1)}, bf16[64,64,64,1]{2,1,3,0:T(8,128)(2,1)}, u32[]{:S(2)}) copy-start(bf16[64,64,64,1]{2,1,3,0:T(8,128)(2,1)} %constant.205) | copy-start | bytes 1572868
  28.1 0.8 copy-start.7
  31.2 0.7 copy-start.9
  31.3 0.8 copy-start.12
  31.5 2.1 %copy-start.10 = (f32[3,16,8]{1,2,0:T(8,128)S(1)}, f32[3,16,8]{1,2,0:T(8,128)}, u32[]{:S(2)}) copy-start(f32[3,16,8]{1,2,0:T(8,128)} %param.19) | copy-start | bytes 4612
  31.6 2.6 %copy-start.13 = (f32[3,4]{1,0:T(4,128)S(1)}, f32[3,4]{1,0:T(4,128)}, u32[]{:S(2)}) copy-start(f32[3,4]{1,0:T(4,128)} %constant.128) | copy-start | bytes 148
  37.1 31.1 %copy-start.8 = (bf16[128,128,1]{1,0,2:T(8,128)(2,1)S(1)}, bf16[128,128,1]{1,0,2:T(8,128)(2,1)}, u32[]{:S(2)}) copy-start(bf16[128,128,1]{1,0,2:T(8,128)(2,1)} %constant.206) | copy-start | bytes 98308
  37.1 31.1 %copy-start.16 = (f32[64]{0:T(128)S(1)}, f32[64]{0:T(128)}, u32[]{:S(2)}) copy-start(f32[64]{0:T(128)} %constant.116.clone) | copy-start | bytes 772
  58.1 19.5 %all-to-all-start.1 = ((f32[128,2,13]{2,1,0:T(2,128)}), f32[128,2,13]{2,1,0:T(2,128)S(1)}, u32[]{:S(2)}, u32[]{:S(2)}) async-start(f32[128,2,13]{2,1,0:T(2,128)} %bitcast.38), calls=%async_computation.1 | async-start | bytes 262144 | tf_op jit(solution)/shard_map/all_to_all | solution.py:290
  69.8 9.1 %copy-start.3 = (f32[16,64,128]{2,1,0:T(8,128)S(1)}, f32[16,64,128]{2,1,0:T(8,128)}, u32[]{:S(2)}) copy-start(f32[16,64,128]{2,1,0:T(8,128)} %get-tuple-element.44) | copy-start | bytes 1572868
  71.0 8.6 %copy-start.5 = (bf16[64,64,64]{2,1,0:T(8,128)(2,1)S(1)}, bf16[64,64,64]{2,1,0:T(8,128)(2,1)}, u32[]{:S(2)}) copy-start(bf16[64,64,64]{2,1,0:T(8,128)(2,1)} %constant.207) | copy-start | bytes 1572868

commit v5 on v4

--- a/solution.py
+++ b/solution.py
@@ -266,7 +266,7 @@
     cell_table = cell_tables(nlat, nlon, point_count)
     partial = near_field(entry_table, near_grid, cell_table, readers, point_count)
     partial, traction_grid = lax.optimization_barrier((partial, traction_grid))
-    sums = jnp.sum(partial, axis=3)
+    sums = partial
     contribution = (
         sums[:, :3] + jnp.transpose(target_point, (0, 2, 1)) * sums[:, 3:]
     ) / (8.0 * math.pi)
@@ -342,7 +342,7 @@
     return jnp.asarray(table, dtype=jnp.float32)
 
 
-def near_kernel(points, t_ref, g_ref, c_ref, o_ref, s_ref):
+def near_kernel(points, t_ref, g_ref, c_ref, f_ref, s_ref, o_ref):
     drop = pl.program_id(0)
     entries = o_ref.shape[2] // points
     width = 3 + 2 * points
@@ -387,6 +387,13 @@
         return carry
 
     lax.fori_loop(0, entries, body, 0)
+    rows = o_ref.shape[1] * o_ref.shape[2]
+    table = o_ref[0].reshape(rows, o_ref.shape[3])
+    ones = jnp.ones((8, o_ref.shape[3]), jnp.float32)
+    totals = lax.dot_general(
+        ones, table, (((1,), (1,)), ((), ())), precision=HIGH, preferred_element_type=jnp.float32
+    )
+    f_ref[0] = totals[0:1, :]
 
 
 def near_field(entry_table, near_grid, cell_table, readers, points):
@@ -401,13 +408,16 @@
             pl.BlockSpec((1, fields, nlat, nlon), lambda s: (s, 0, 0, 0)),
             pl.BlockSpec(cell_table.shape, lambda s: (0, 0, 0)),
         ],
-        out_specs=pl.BlockSpec((1, 4, targets, nlon), lambda s: (s, 0, 0, 0)),
-        out_shape=jax.ShapeDtypeStruct((drops, 4, targets, nlon), jnp.float32),
-        scratch_shapes=[pltpu.VMEM((4, nlat, nlon), jnp.float32)],
+        out_specs=pl.BlockSpec((1, 1, 4 * targets), lambda s: (s, 0, 0)),
+        out_shape=jax.ShapeDtypeStruct((drops, 1, 4 * targets), jnp.float32),
+        scratch_shapes=[
+            pltpu.VMEM((4, nlat, nlon), jnp.float32),
+            pltpu.VMEM((1, 4, targets, nlon), jnp.float32),
+        ],
         cost_estimate=pl.CostEstimate(
             flops=24 * cells, transcendentals=cells, bytes_accessed=2 * drops * fields * nlat * nlon
         ),
-    )(entry_table, near_grid, cell_table)
+    )(entry_table, near_grid, cell_table).reshape(drops, 4, targets)
 
 
 def solution(mesh):

time: 82 us -> 85.8 us (1.046)
  Pallas kernels: 18.1 us -> 21.3 us
    pallas_call x1, Pallas kernels: 18.1 us -> 21.3 us  [near_field(): pl.pallas_call(functools.partial(near_kernel, points), grid=(drops,), in_...]
    reduce_sum x1 -> x0, other arithmetic: 1.57 us -> none  [per_device(): sums = jnp.sum(partial, axis=3)]
    pallas_call x0 -> x1, other arithmetic: none -> 1.36 us  [near_field(): pl.pallas_call(functools.partial(near_kernel, points), grid=(drops,), in_...]
    add x1, other arithmetic: 0.06 us -> 1.01 us  [per_device(): partial_surface + from_partner(partial_surface.astype(jnp.bfloat16), 'row...]
  transfers between devices with their start and end apart: 3 -> 3, of which waited for: 1 -> 1; matrix products, arithmetic and copies ran while one was open for 34% -> 32% of each run, Pallas kernels for 22% -> 25%
where the time goes in v5:
time: 85.8 us; the launch traced here: 84.5 us
  Pallas kernels  21.3 us (25%)
  starting transfers between devices  21.2 us (25%)
  local copies, waits for them, and re-layouts  18.6 us (22%)
  matrix products  9.59 us (11%)
  other arithmetic  6.96 us (8%)
  waiting for transfers between devices  5.54 us (6%)
  between operations  1.27 us (1%)
    pallas_call x1, Pallas kernels, near_field(): pl.pallas_call(functools.partial(near_kernel, points), grid=(drops,), in_...  21.3 us
    all_to_all x1, starting transfers between devices, per_device(): lax.all_to_all(jnp.broadcast_to(own_points.reshape(1, -1), (devices, drop...  11.2 us
    all_to_all x1, starting transfers between devices, per_device(): lax.all_to_all(outgoing.reshape(devices, capacity, record.shape[1]), ('ro...  10.1 us
    reshape x2, local copies, waits for them, and re-layouts, per_device(): prepared.reshape(drop_count * 4, degrees, 2, degrees)  7.52 us
    all_to_all x1, waiting for transfers between devices, per_device(): lax.all_to_all(outgoing.reshape(devices, capacity, record.shape[1]), ('ro...  5.54 us
    dot_general x1, matrix products, per_device(): jnp.einsum('mcnj,cmk->njk', batched, fourier.reshape(2, degrees, nlon), p...  2.34 us
    dot_general x1, matrix products, per_device(): jnp.dot((coeffs[:, 0] * keep_mask).reshape(drop_count, degrees * coef_wid...  2.22 us
  transfers between devices with their start and end apart: 3, of which 1 were waited for; matrix products, arithmetic and copies ran while one was open for 32% of the time, Pallas kernels for 25%

profile of v5, /device:TPU:0, one launch (start us, length us, event | category | flops | bytes accessed | tf_op | source)
XLA Modules:
  0.0 84.5 jit_solution(16543078265992395712)
XLA Ops:
  0.7 0.8 fusion.56
  1.5 1.1 %slice.69 = f32[16,1,64,128]{3,2,1,0:T(8,128)S(1)} slice(f32[16,3,64,128]{3,2,1,0:T(8,128)} %param.14), slice={[0:16], [0:1], [0:64], [0:128]} | slice | bytes 1048576 | tf_op jit(solution)/shard_map/slice | solution.py:195
  2.5 0.2 mul.331
  2.7 2.2 %fusion.5 = bf16[16,4]{0,1:T(4,128)(2,1)S(1)} fusion(f32[8192,4]{0,1:T(4,128)} %constant.118.clone, f32[2,8,64,128]{3,2,1,0:T(8,128)S(1)} %bitcast.144, f32[2,8,64,128]{3,2,1,0:T(8,128)S(1)} %bitcast.143, f32[8192]{0:T(1024)S(1)} %get-tuple-element.39), kind=kOutput, calls=%fused_computation.11 | convolution fusion | flops 3407936 | bytes 1212544 | tf_op jit(solution)/shard_map/dot_general | solution.py:194
  5.0 0.1 copy.133
  5.1 0.1 broadcast_in_dim.4
  5.2 0.7 broadcast_in_dim.5
  5.9 11.2 %all-to-all-start = ((bf16[128,1,64]{2,1,0:T(2,128)(2,1)}), bf16[128,1,64]{2,1,0:T(2,128)(2,1)S(1)}, u32[]{:S(2)}, u32[]{:S(2)}) async-start(bf16[128,1,64]{2,1,0:T(2,128)(2,1)} %broadcast_in_dim.5), calls=%async_computation | async-start | bytes 131072 | tf_op jit(solution)/shard_map/all_to_all | solution.py:237
  17.3 0.1 copy.175
  17.4 0.1 copy.176
  17.5 0.1 copy.174
  17.8 0.4 convolution_bitcast_fusion.2
  18.2 1.2 %fusion.66 = (bf16[16,64,128]{2,1,0:T(8,128)(2,1)}, f32[16,64,128]{2,1,0:T(8,128)}) fusion(bf16[2,64,128]{2,1,0:T(8,128)(2,1)S(1)} %copy-done.11, s32[]{:T(128)S(6)} %select_n.48, bf16[16,64,2,32]{1,0,2,3:T(8,128)(2,1)S(1)} %convolution_bitcast_fusion.2), kind=kOutput, calls=%fused_computation.117 | convolution fusion | flops 16908288 | bytes 1064964 | tf_op jit(solution)/shard_map/njw,wk->njk/dot_general | solution.py:134
  19.4 0.4 broadcast_multiply_fusion
  19.8 0.1 pad_maximum_fusion
  19.9 1.9 %reshape.247 = bf16[64,64,2,64]{3,2,1,0:T(2,128)(2,1)} reshape(bf16[16,4,64,128]{3,2,1,0:T(8,128)(2,1)S(1)} %pad_maximum_fusion) | data formatting | bytes 2097152 | tf_op jit(solution)/shard_map/reshape | solution.py:203
  21.8 5.7 %copy.139 = bf16[64,64,2,64]{1,0,2,3:T(8,128)(2,1)S(1)} copy(bf16[64,64,2,64]{3,2,1,0:T(2,128)(2,1)} %reshape.247) | data formatting | bytes 2097152 | tf_op jit(solution)/shard_map/reshape | solution.py:203
  27.5 0.7 fusion.67
  28.2 2.3 %fusion.2 = f32[16,4,64,128]{3,2,1,0:T(8,128)S(1)} fusion(bf16[2,64,128,1,1]{2,1,0,4,3:T(8,128)(2,1)S(1)} %copy-done.7, bf16[16,4,64,2,64]{2,1,0,3,4:T(4,128)(2,1)S(1)} %bitcast.142), kind=kOutput, calls=%fused_computation.3 | convolution fusion | flops 134217728 | bytes 3178496 | tf_op jit(solution)/shard_map/mcnj,cmk->njk/dot_general | solution.py:206
  30.6 0.3 fusion.23
  30.9 0.2 fusion.16
  31.1 0.2 copy-done.9
  31.4 0.1 fusion.42
  31.5 0.2 reduce_window_sum.11
  31.7 0.2 select_reduce_fusion
  32.0 0.8 pad_maximum_fusion.1.g_ref
  33.1 0.1 add.129
  33.2 0.1 add.130
  33.3 0.1 add.131
  33.5 0.1 mul.339
  33.7 0.1 convert_element_type.71
  33.8 0.2 reduce.1
  33.9 0.6 reshape.244
  34.6 0.4 fusion.10
  34.9 0.1 copy.135
  35.0 0.1 reshape.245
  35.4 0.2 copy.138
  35.6 0.8 reshape.246.t_ref
  36.4 21.3 %shard_map.157 = f32[16,1,128]{2,1,0:T(1,128)} custom-call(f32[1408]{0:T(1024)} %reshape.246.t_ref, bf16[16,2,64,128]{3,2,1,0:T(8,128)(2,1)} %pad_maximum_fusion.1.g_ref, f32[8,64,128]{2,1,0:T(8,128)} %constant.119.clone.c_ref), custom_call_target="tpu_custom_call" | custom-call | flops 100663296 | bytes 524288 | tf_op jit(solution)/shard_map/pallas_call | solution.py:403
  57.7 0.5 broadcast.234
  58.2 1.4 %reduce.7 = f32[16,128]{1,0:T(8,128)S(1)} reduce(f32[16,1,128]{2,1,0:T(1,128)} %shard_map.157, f32[]{:T(128)} %broadcast.234), dimensions={1}, to_apply=%pallas_call.3.reduce_sub_computation.3 | reduce | bytes 16388 | tf_op jit(solution)/shard_map/pallas_call | solution.py:403
  59.8 0.1 copy.159
  59.9 0.1 reshape.257
  60.0 1.0 %fusion.38 = f32[256,13]{1,0:T(8,128)} fusion(s32[128]{0:T(128)S(1)} %multiply_add_fusion.2, f32[128,1]{0,1:T(1,128)S(1)} %convert_element_type.71, f32[128,12]{0,1:T(8,128)S(1)} %reshape.257), kind=kOutput, calls=%fused_computation.66 | convolution fusion | flops 5179008 | bytes 20480 | tf_op jit(solution)/shard_map/dot_general | solution.py:289
  61.0 10.1 %all-to-all-start.1 = ((f32[128,2,13]{2,1,0:T(2,128)}), f32[128,2,13]{2,1,0:T(2,128)S(1)}, u32[]{:S(2)}, u32[]{:S(2)}) async-start(f32[128,2,13]{2,1,0:T(2,128)} %bitcast.38), calls=%async_computation.1 | async-start | bytes 262144 | tf_op jit(solution)/shard_map/all_to_all | solution.py:290
  71.1 0.2 convolution_multiply_fusion
  71.3 0.2 reshape.250
  71.5 0.7 copy.144
  72.2 0.4 convolution_bitcast_fusion
  72.6 0.7 copy.145
  73.3 0.6 reshape.251
  73.9 1.0 %multiply_multiply_fusion.5 = f32[16,64,128]{2,1,0:T(8,128)} fusion(f32[16,64,128]{2,1,0:T(8,128)S(1)} %reshape.251, f32[64,128]{1,0:T(8,128)S(1)} %get-tuple-element.38, f32[16,64]{1,0:T(8,128)S(1)} %fusion.56), kind=kLoop, calls=%fused_computation.45 | loop fusion | flops 262144 | bytes 1085440 | tf_op jit(solution)/shard_map/mul | solution.py:303
  74.9 5.5 %all-to-all-done.1 = f32[128,2,13]{2,1,0:T(2,128)S(1)} async-done(((f32[128,2,13]{2,1,0:T(2,128)}), f32[128,2,13]{2,1,0:T(2,128)S(1)}, u32[]{:S(2)}, u32[]{:S(2)}) %all-to-all-start.1) | async-done | bytes 13344 | tf_op jit(solution)/shard_map/all_to_all | solution.py:290
  80.4 0.2 slice_reduce_fusion
  80.6 0.3 fusion.31
  80.9 0.1 copy.163
  81.0 0.7 reshape.261
  81.7 1.0 %convert_add_fusion = f32[16,64,128]{2,1,0:T(8,128)S(1)} fusion(f32[16,64,128]{2,1,0:T(8,128)S(1)} %copy-done.3, bf16[16,64,128]{2,1,0:T(8,128)(2,1)} %collective-permute-done), kind=kLoop, calls=%fused_computation.44 | loop fusion | flops 262144 | bytes 1310720 | tf_op jit(solution)/shard_map/add | solution.py:229
  82.7 0.2 convolution_multiply_fusion.1
  83.0 0.1 reshape.253
  83.1 0.2 constant_dynamic-slice_fusion
  83.3 0.1 copy.180
  83.4 0.3 convolution_bitcast_fusion.3
  83.7 0.8 copy.164
  (70 shorter events, 1.6 us)
Async XLA Ops:
  0.6 31.3 %copy-start = (f32[256,2]{0,1:T(2,128)S(1)}, f32[256,2]{0,1:T(2,128)}, u32[]{:S(2)}) copy-start(f32[256,2]{0,1:T(2,128)} %param.18) | copy-start | bytes 6148
  0.6 16.6 %copy-start.6 = (f32[4,3,64,64]{3,2,1,0:T(8,128)S(1)}, f32[4,3,64,64]{3,2,1,0:T(8,128)}, u32[]{:S(2)}) copy-start(f32[4,3,64,64]{3,2,1,0:T(8,128)} %param.17) | copy-start | bytes 589828
  2.7 15.0 %copy-start.4 = (bf16[64,64,64]{2,1,0:T(8,128)(2,1)S(1)}, bf16[64,64,64]{2,1,0:T(8,128)(2,1)}, u32[]{:S(2)}) copy-start(bf16[64,64,64]{2,1,0:T(8,128)(2,1)} %constant.211) | copy-start | bytes 1572868
  5.2 13.0 %copy-start.11 = (bf16[2,64,128]{2,1,0:T(8,128)(2,1)S(1)}, bf16[2,64,128]{2,1,0:T(8,128)(2,1)}, u32[]{:S(2)}) copy-start(bf16[2,64,128]{2,1,0:T(8,128)(2,1)} %constant.212) | copy-start | bytes 98308
  5.9 27.9 %all-to-all-start = ((bf16[128,1,64]{2,1,0:T(2,128)(2,1)}), bf16[128,1,64]{2,1,0:T(2,128)(2,1)S(1)}, u32[]{:S(2)}, u32[]{:S(2)}) async-start(bf16[128,1,64]{2,1,0:T(2,128)(2,1)} %broadcast_in_dim.5), calls=%async_computation | async-start | bytes 131072 | tf_op jit(solution)/shard_map/all_to_all | solution.py:237
  17.3 2.1 %copy-start.2 = (f32[16,3,64,128]{3,2,1,0:T(8,128)S(1)}, f32[16,3,64,128]{3,2,1,0:T(8,128)}, u32[]{:S(2)}) copy-start(f32[16,3,64,128]{3,2,1,0:T(8,128)} %param.14) | copy-start | bytes 4718596
  19.4 62.3 %collective-permute-start = (bf16[16,64,128]{2,1,0:T(8,128)(2,1)}, bf16[16,64,128]{2,1,0:T(8,128)(2,1)}, u32[]{:S(2)}, u32[]{:S(2)}) collective-permute-start(bf16[16,64,128]{2,1,0:T(8,128)(2,1)} %get-tuple-element.40), channel_id=1, source_target_pairs={{0,16},{16,0},{32,48},{48,32},{64,80},{80,64},{96,112},{112,96},{1... | collective-permute-start | bytes 786440 | tf_op jit(solution)/shard_map/ppermute | solution.py:24
  21.8 5.7 %copy-start.14 = (f32[16,2]{0,1:T(2,128)S(1)}, f32[16,2]{0,1:T(2,128)}, u32[]{:S(2)}) copy-start(f32[16,2]{0,1:T(2,128)} %param.16) | copy-start | bytes 388
  21.8 5.7 %copy-start.1 = (bf16[64,64,64,1]{2,1,3,0:T(8,128)(2,1)S(1)}, bf16[64,64,64,1]{2,1,3,0:T(8,128)(2,1)}, u32[]{:S(2)}) copy-start(bf16[64,64,64,1]{2,1,3,0:T(8,128)(2,1)} %constant.209) | copy-start | bytes 1572868
  27.5 0.8 copy-start.7
  30.6 0.7 copy-start.9
  30.6 0.8 copy-start.12
  30.9 2.1 %copy-start.10 = (f32[3,16,8]{1,2,0:T(8,128)S(1)}, f32[3,16,8]{1,2,0:T(8,128)}, u32[]{:S(2)}) copy-start(f32[3,16,8]{1,2,0:T(8,128)} %param.19) | copy-start | bytes 4612
  30.9 2.6 %copy-start.13 = (f32[3,4]{1,0:T(4,128)S(1)}, f32[3,4]{1,0:T(4,128)}, u32[]{:S(2)}) copy-start(f32[3,4]{1,0:T(4,128)} %constant.128) | copy-start | bytes 148
  36.4 34.6 %copy-start.8 = (bf16[128,128,1]{1,0,2:T(8,128)(2,1)S(1)}, bf16[128,128,1]{1,0,2:T(8,128)(2,1)}, u32[]{:S(2)}) copy-start(bf16[128,128,1]{1,0,2:T(8,128)(2,1)} %constant.210) | copy-start | bytes 98308
  36.4 34.6 %copy-start.15 = (f32[64]{0:T(128)S(1)}, f32[64]{0:T(128)}, u32[]{:S(2)}) copy-start(f32[64]{0:T(128)} %constant.116.clone) | copy-start | bytes 772
  61.0 19.5 %all-to-all-start.1 = ((f32[128,2,13]{2,1,0:T(2,128)}), f32[128,2,13]{2,1,0:T(2,128)S(1)}, u32[]{:S(2)}, u32[]{:S(2)}) async-start(f32[128,2,13]{2,1,0:T(2,128)} %bitcast.38), calls=%async_computation.1 | async-start | bytes 262144 | tf_op jit(solution)/shard_map/all_to_all | solution.py:290
  72.6 9.1 %copy-start.3 = (f32[16,64,128]{2,1,0:T(8,128)S(1)}, f32[16,64,128]{2,1,0:T(8,128)}, u32[]{:S(2)}) copy-start(f32[16,64,128]{2,1,0:T(8,128)} %get-tuple-element.41) | copy-start | bytes 1572868
  73.9 9.5 %copy-start.5 = (bf16[64,64,64]{2,1,0:T(8,128)(2,1)S(1)}, bf16[64,64,64]{2,1,0:T(8,128)(2,1)}, u32[]{:S(2)}) copy-start(bf16[64,64,64]{2,1,0:T(8,128)(2,1)} %constant.211) | copy-start | bytes 1572868

commit v6 on v4

--- a/solution.py
+++ b/solution.py
@@ -9,7 +9,6 @@
 from jax.experimental.pallas import tpu as pltpu
 from jax.sharding import PartitionSpec as P
 
-HIGH = lax.Precision.HIGHEST
 SPECTRAL = lax.Precision.DEFAULT
 SOFTENING = 0.04
 
@@ -194,7 +193,7 @@
     point_surface = jnp.dot(
         (coeffs[:, 0] * keep_mask).reshape(drop_count, degrees * coef_width),
         point_weight,
-        precision=lax.Precision.HIGH,
+        precision=lax.Precision.DEFAULT,
     )
     own_points = jnp.exp(point_surface).astype(jnp.bfloat16)
     batched = jnp.einsum(
@@ -247,7 +246,9 @@
     pick = (target[:, None] == jnp.arange(total_drops, dtype=jnp.int32)[None, :]).astype(
         jnp.float32
     )
-    target_radius = jnp.dot(pick, all_points.astype(jnp.float32), precision=HIGH)
+    target_radius = jnp.dot(
+        pick, all_points.astype(jnp.float32), precision=lax.Precision.DEFAULT
+    )
     target_point = separation.reshape(3, drop_count * readers)[:, :, None] + (
         target_radius[None] * target_normal[:, None, :]
     )
@@ -286,7 +287,7 @@
     record = jnp.concatenate(
         [contribution, reader_slot.reshape(-1, 1).astype(jnp.float32)], axis=1
     )
-    outgoing = jnp.dot(jnp.transpose(place), record, precision=HIGH)
+    outgoing = jnp.dot(jnp.transpose(place), record, precision=lax.Precision.HIGH)
     incoming = lax.all_to_all(
         outgoing.reshape(devices, capacity, record.shape[1]),
         ("row", "col"),
@@ -297,7 +298,9 @@
     slot_pick = (
         incoming[:, -1:] == jnp.arange(drop_count, dtype=jnp.float32)[None, :]
     ).astype(jnp.float32)
-    mine = jnp.dot(jnp.transpose(slot_pick), incoming[:, :-1], precision=HIGH)
+    mine = jnp.dot(
+        jnp.transpose(slot_pick), incoming[:, :-1], precision=lax.Precision.HIGH
+    )
     near_velocity = jnp.transpose(mine.reshape(drop_count, 3, point_count), (1, 0, 2))
     traction_coeffs = (
         analysis_legendre(analysis_fourier(traction_grid, fourier, quad_weight), legendre)

time: 82 us -> 81.3 us (level)
  transfers between devices with their start and end apart: 3 -> 3, of which waited for: 1 -> 1; matrix products, arithmetic and copies ran while one was open for 34% -> 34% of each run, Pallas kernels for 22% -> 23%
where the time goes in v6:
time: 81.3 us; the launch traced here: 80.1 us
  starting transfers between devices  21.2 us (26%)
  Pallas kernels  18.1 us (22%)
  local copies, waits for them, and re-layouts  18 us (22%)
  matrix products  8.95 us (11%)
  other arithmetic  6.87 us (8%)
  waiting for transfers between devices  5.54 us (7%)
  between operations  1.28 us (2%)
    pallas_call x1, Pallas kernels, near_field(): pl.pallas_call(functools.partial(near_kernel, points), grid=(drops,), in_...  18.1 us
    all_to_all x1, starting transfers between devices, per_device(): lax.all_to_all(jnp.broadcast_to(own_points.reshape(1, -1), (devices, drop...  11.2 us
    all_to_all x1, starting transfers between devices, per_device(): lax.all_to_all(outgoing.reshape(devices, capacity, record.shape[1]), ('ro...  10.1 us
    reshape x2, local copies, waits for them, and re-layouts, per_device(): prepared.reshape(drop_count * 4, degrees, 2, degrees)  7.52 us
    all_to_all x1, waiting for transfers between devices, per_device(): lax.all_to_all(outgoing.reshape(devices, capacity, record.shape[1]), ('ro...  5.54 us
    dot_general x1, matrix products, per_device(): jnp.einsum('mcnj,cmk->njk', batched, fourier.reshape(2, degrees, nlon), p...  2.34 us
    dot_general x1, matrix products, per_device(): jnp.dot((coeffs[:, 0] * keep_mask).reshape(drop_count, degrees * coef_wid...  1.65 us
  transfers between devices with their start and end apart: 3, of which 1 were waited for; matrix products, arithmetic and copies ran while one was open for 34% of the time, Pallas kernels for 23%

profile of v6, /device:TPU:0, one launch (start us, length us, event | category | flops | bytes accessed | tf_op | source)
XLA Modules:
  0.0 80.1 jit_solution(4186127947095502493)
XLA Ops:
  0.7 0.8 fusion.56
  1.5 1.1 %slice.69 = f32[16,1,64,128]{3,2,1,0:T(8,128)S(1)} slice(f32[16,3,64,128]{3,2,1,0:T(8,128)} %param.14), slice={[0:16], [0:1], [0:64], [0:128]} | slice | bytes 1048576 | tf_op jit(solution)/shard_map/slice | solution.py:194
  2.5 0.2 mul.331
  2.7 1.6 %fusion.5 = bf16[16,4]{0,1:T(4,128)(2,1)S(1)} fusion(bf16[8192,4]{0,1:T(4,128)(2,1)} %constant.204, f32[2,8,64,128]{3,2,1,0:T(8,128)S(1)} %bitcast.145, f32[2,8,64,128]{3,2,1,0:T(8,128)S(1)} %bitcast.144, f32[8192]{0:T(1024)S(1)} %get-tuple-element.42), kind=kOutput, calls=%fused_computation.11 | convolution fusion | flops 1310784 | bytes 1147008 | tf_op jit(solution)/shard_map/dot_general | solution.py:193
  4.4 0.1 copy.169
  4.5 0.1 broadcast_in_dim.4
  4.6 0.7 broadcast_in_dim.5
  5.3 11.2 %all-to-all-start = ((bf16[128,1,64]{2,1,0:T(2,128)(2,1)}), bf16[128,1,64]{2,1,0:T(2,128)(2,1)S(1)}, u32[]{:S(2)}, u32[]{:S(2)}) async-start(bf16[128,1,64]{2,1,0:T(2,128)(2,1)} %broadcast_in_dim.5), calls=%async_computation | async-start | bytes 131072 | tf_op jit(solution)/shard_map/all_to_all | solution.py:236
  16.7 0.1 copy.211
  16.8 0.1 copy.212
  16.9 0.1 copy.210
  17.2 0.4 convolution_bitcast_fusion.2
  17.6 1.2 %fusion.66 = (bf16[16,64,128]{2,1,0:T(8,128)(2,1)}, f32[16,64,128]{2,1,0:T(8,128)}) fusion(bf16[2,64,128]{2,1,0:T(8,128)(2,1)S(1)} %copy-done.11, s32[]{:T(128)S(6)} %select_n.48, bf16[16,64,2,32]{1,0,2,3:T(8,128)(2,1)S(1)} %convolution_bitcast_fusion.2), kind=kOutput, calls=%fused_computation.117 | convolution fusion | flops 16908288 | bytes 1064964 | tf_op jit(solution)/shard_map/njw,wk->njk/dot_general | solution.py:133
  18.8 1.0 %broadcast_multiply_fusion = (bf16[16,1,64,128]{3,2,1,0:T(8,128)(2,1)S(1)}, bf16[16,1,64,128]{3,2,1,0:T(8,128)(2,1)S(1)}, bf16[16,1,64,128]{3,2,1,0:T(8,128)(2,1)S(1)}, bf16[16,1,64,128]{3,2,1,0:T(8,128)(2,1)S(1)}) fusion(f32[64]{0:T(128)S(1)} %get-tuple-element.45, f32[16,64]{1,0:T(8,128)S(1)} %fusion.56, f32[64,128]{1,0:T(8,128)S(1)} %get-tuple-element.41, ...), kind=kLoop, calls=%fused_computation.47 | loop fusion | flops 1572864 | bytes 2658816 | tf_op jit(solution)/shard_map/mul | solution.py:161
  19.8 0.1 pad_maximum_fusion
  20.0 1.9 %reshape.244 = bf16[64,64,2,64]{3,2,1,0:T(2,128)(2,1)} reshape(bf16[16,4,64,128]{3,2,1,0:T(8,128)(2,1)S(1)} %pad_maximum_fusion) | data formatting | bytes 2097152 | tf_op jit(solution)/shard_map/reshape | solution.py:202
  21.8 5.7 %copy.175 = bf16[64,64,2,64]{1,0,2,3:T(8,128)(2,1)S(1)} copy(bf16[64,64,2,64]{3,2,1,0:T(2,128)(2,1)} %reshape.244) | data formatting | bytes 2097152 | tf_op jit(solution)/shard_map/reshape | solution.py:202
  27.6 0.7 fusion.67
  28.3 2.3 %fusion.2 = f32[16,4,64,128]{3,2,1,0:T(8,128)S(1)} fusion(bf16[2,64,128,1,1]{2,1,0,4,3:T(8,128)(2,1)S(1)} %copy-done.7, bf16[16,4,64,2,64]{2,1,0,3,4:T(4,128)(2,1)S(1)} %bitcast.143), kind=kOutput, calls=%fused_computation.3 | convolution fusion | flops 134217728 | bytes 3178496 | tf_op jit(solution)/shard_map/mcnj,cmk->njk/dot_general | solution.py:205
  30.7 0.3 fusion.23
  31.0 0.2 fusion.16
  31.2 0.2 copy-done.9
  31.4 0.1 reshape.251
  31.5 0.1 fusion.42
  31.6 0.2 reduce_window_sum.11
  31.8 0.2 select_reduce_fusion
  32.1 0.8 %pad_maximum_fusion.1.g_ref = bf16[16,2,64,128]{3,2,1,0:T(8,128)(2,1)} fusion(bf16[16,1,64,128]{3,2,1,0:T(8,128)(2,1)S(1)} %get-tuple-element.27, bf16[16,1,64,128]{3,2,1,0:T(8,128)(2,1)S(1)} %get-tuple-element.26), kind=kLoop, calls=%fused_computation.37 | loop fusion | flops 262144 | bytes 1048576 | tf_op jit(solution)/shard_map/stack | solution.py:232
  33.0 0.1 eq.62
  33.2 0.1 add.129
  33.3 0.1 add.130
  33.4 0.1 add.131
  33.5 0.1 mul.339
  33.7 0.1 convert_element_type.71
  33.8 0.2 reduce.1
  34.0 0.6 reshape.241
  34.6 0.4 fusion.10
  35.0 0.1 copy.171
  35.1 0.1 reshape.242
  35.5 0.2 copy.174
  35.7 0.8 reshape.243.t_ref
  36.5 18.1 %shard_map.157 = f32[16,4,32,128]{3,2,1,0:T(8,128)} custom-call(f32[1408]{0:T(1024)} %reshape.243.t_ref, bf16[16,2,64,128]{3,2,1,0:T(8,128)(2,1)} %pad_maximum_fusion.1.g_ref, f32[8,64,128]{2,1,0:T(8,128)} %constant.119.clone.c_ref), custom_call_target="tpu_custom_call" | custom-call | flops 100663296 | bytes 524288 | tf_op jit(solution)/shard_map/pallas_call | solution.py:399
  54.6 1.6 %reduce_sum.29 = f32[16,4,32]{2,1,0:T(4,128)S(1)} reduce(f32[16,4,32,128]{3,2,1,0:T(8,128)} %shard_map.157, f32[]{:T(128)} %constant.95.clone.1), dimensions={3}, to_apply=%region_3.4 | reduce | flops 260096 | bytes 1056772 | tf_op jit(solution)/shard_map/reduce_sum | solution.py:270
  56.3 0.1 copy.195
  56.4 0.1 reshape.253
  56.5 1.0 %fusion.38 = f32[256,13]{1,0:T(8,128)} fusion(s32[128]{0:T(128)S(1)} %multiply_add_fusion.2, f32[128,1]{0,1:T(1,128)S(1)} %convert_element_type.71, f32[128,12]{0,1:T(8,128)S(1)} %reshape.253), kind=kOutput, calls=%fused_computation.66 | convolution fusion | flops 2623104 | bytes 20480 | tf_op jit(solution)/shard_map/dot_general | solution.py:290
  57.5 10.1 %all-to-all-start.1 = ((f32[128,2,13]{2,1,0:T(2,128)}), f32[128,2,13]{2,1,0:T(2,128)S(1)}, u32[]{:S(2)}, u32[]{:S(2)}) async-start(f32[128,2,13]{2,1,0:T(2,128)} %bitcast.38), calls=%async_computation.1 | async-start | bytes 262144 | tf_op jit(solution)/shard_map/all_to_all | solution.py:291
  67.6 0.2 convolution_multiply_fusion
  67.8 0.2 reshape.246
  68.1 0.7 copy.180
  68.8 0.4 convolution_bitcast_fusion
  69.2 0.7 copy.181
  69.8 0.6 reshape.247
  70.4 1.0 %multiply_multiply_fusion.5 = f32[16,64,128]{2,1,0:T(8,128)} fusion(f32[16,64,128]{2,1,0:T(8,128)S(1)} %reshape.247, f32[64,128]{1,0:T(8,128)S(1)} %get-tuple-element.41, f32[16,64]{1,0:T(8,128)S(1)} %fusion.56), kind=kLoop, calls=%fused_computation.45 | loop fusion | flops 262144 | bytes 1085440 | tf_op jit(solution)/shard_map/mul | solution.py:306
  71.4 5.5 %all-to-all-done.1 = f32[128,2,13]{2,1,0:T(2,128)S(1)} async-done(((f32[128,2,13]{2,1,0:T(2,128)}), f32[128,2,13]{2,1,0:T(2,128)S(1)}, u32[]{:S(2)}, u32[]{:S(2)}) %all-to-all-start.1) | async-done | bytes 13344 | tf_op jit(solution)/shard_map/all_to_all | solution.py:291
  77.0 0.2 slice_reduce_fusion
  77.1 0.3 fusion.31
  77.4 0.1 copy.199
  77.5 0.7 reshape.257
  78.3 0.2 convolution_multiply_fusion.1
  78.5 0.1 reshape.249
  78.6 0.2 constant_dynamic-slice_fusion
  78.8 0.1 copy.216
  79.0 0.3 convolution_bitcast_fusion.3
  79.3 0.8 copy.200
  (69 shorter events, 1.4 us)
Async XLA Ops:
  0.6 31.4 %copy-start = (f32[256,2]{0,1:T(2,128)S(1)}, f32[256,2]{0,1:T(2,128)}, u32[]{:S(2)}) copy-start(f32[256,2]{0,1:T(2,128)} %param.18) | copy-start | bytes 6148
  0.6 16.0 %copy-start.6 = (f32[4,3,64,64]{3,2,1,0:T(8,128)S(1)}, f32[4,3,64,64]{3,2,1,0:T(8,128)}, u32[]{:S(2)}) copy-start(f32[4,3,64,64]{3,2,1,0:T(8,128)} %param.17) | copy-start | bytes 589828
  2.7 14.5 %copy-start.4 = (bf16[64,64,64]{2,1,0:T(8,128)(2,1)S(1)}, bf16[64,64,64]{2,1,0:T(8,128)(2,1)}, u32[]{:S(2)}) copy-start(bf16[64,64,64]{2,1,0:T(8,128)(2,1)} %constant.208) | copy-start | bytes 1572868
  4.6 13.0 %copy-start.11 = (bf16[2,64,128]{2,1,0:T(8,128)(2,1)S(1)}, bf16[2,64,128]{2,1,0:T(8,128)(2,1)}, u32[]{:S(2)}) copy-start(bf16[2,64,128]{2,1,0:T(8,128)(2,1)} %constant.209) | copy-start | bytes 98308
  5.3 28.5 %all-to-all-start = ((bf16[128,1,64]{2,1,0:T(2,128)(2,1)}), bf16[128,1,64]{2,1,0:T(2,128)(2,1)S(1)}, u32[]{:S(2)}, u32[]{:S(2)}) async-start(bf16[128,1,64]{2,1,0:T(2,128)(2,1)} %broadcast_in_dim.5), calls=%async_computation | async-start | bytes 131072 | tf_op jit(solution)/shard_map/all_to_all | solution.py:236
  16.5 2.3 %copy-start.14 = (f32[64]{0:T(128)}, f32[64]{0:T(128)S(1)}, u32[]{:S(2)}) copy-start(f32[64]{0:T(128)S(1)} %get-tuple-element.46) | copy-start | bytes 772
  16.7 2.1 %copy-start.2 = (f32[16,3,64,128]{3,2,1,0:T(8,128)S(1)}, f32[16,3,64,128]{3,2,1,0:T(8,128)}, u32[]{:S(2)}) copy-start(f32[16,3,64,128]{3,2,1,0:T(8,128)} %param.14) | copy-start | bytes 4718596
  18.8 59.4 %collective-permute-start = (bf16[16,64,128]{2,1,0:T(8,128)(2,1)}, bf16[16,64,128]{2,1,0:T(8,128)(2,1)S(1)}, u32[]{:S(2)}, u32[]{:S(2)}) collective-permute-start(bf16[16,64,128]{2,1,0:T(8,128)(2,1)} %get-tuple-element.43), channel_id=1, source_target_pairs={{0,16},{16,0},{32,48},{48,32},{64,80},{80,64},{96,112},{112,96},{1... | collective-permute-start | bytes 786440 | tf_op jit(solution)/shard_map/ppermute | solution.py:23
  21.8 5.7 %copy-start.15 = (f32[16,2]{0,1:T(2,128)S(1)}, f32[16,2]{0,1:T(2,128)}, u32[]{:S(2)}) copy-start(f32[16,2]{0,1:T(2,128)} %param.16) | copy-start | bytes 388
  21.8 5.7 %copy-start.1 = (bf16[64,64,64,1]{2,1,3,0:T(8,128)(2,1)S(1)}, bf16[64,64,64,1]{2,1,3,0:T(8,128)(2,1)}, u32[]{:S(2)}) copy-start(bf16[64,64,64,1]{2,1,3,0:T(8,128)(2,1)} %constant.206) | copy-start | bytes 1572868
  27.5 0.8 copy-start.7
  30.6 0.7 copy-start.9
  30.7 0.8 copy-start.12
  30.9 2.1 %copy-start.10 = (f32[3,16,8]{1,2,0:T(8,128)S(1)}, f32[3,16,8]{1,2,0:T(8,128)}, u32[]{:S(2)}) copy-start(f32[3,16,8]{1,2,0:T(8,128)} %param.19) | copy-start | bytes 4612
  31.0 2.6 %copy-start.13 = (f32[3,4]{1,0:T(4,128)S(1)}, f32[3,4]{1,0:T(4,128)}, u32[]{:S(2)}) copy-start(f32[3,4]{1,0:T(4,128)} %constant.128) | copy-start | bytes 148
  36.5 31.1 %copy-start.8 = (bf16[128,128,1]{1,0,2:T(8,128)(2,1)S(1)}, bf16[128,128,1]{1,0,2:T(8,128)(2,1)}, u32[]{:S(2)}) copy-start(bf16[128,128,1]{1,0,2:T(8,128)(2,1)} %constant.207) | copy-start | bytes 98308
  36.5 31.1 %copy-start.16 = (f32[64]{0:T(128)S(1)}, f32[64]{0:T(128)}, u32[]{:S(2)}) copy-start(f32[64]{0:T(128)} %constant.116.clone) | copy-start | bytes 772
  57.5 19.5 %all-to-all-start.1 = ((f32[128,2,13]{2,1,0:T(2,128)}), f32[128,2,13]{2,1,0:T(2,128)S(1)}, u32[]{:S(2)}, u32[]{:S(2)}) async-start(f32[128,2,13]{2,1,0:T(2,128)} %bitcast.38), calls=%async_computation.1 | async-start | bytes 262144 | tf_op jit(solution)/shard_map/all_to_all | solution.py:291
  69.2 9.1 %copy-start.3 = (f32[16,64,128]{2,1,0:T(8,128)S(1)}, f32[16,64,128]{2,1,0:T(8,128)}, u32[]{:S(2)}) copy-start(f32[16,64,128]{2,1,0:T(8,128)} %get-tuple-element.44) | copy-start | bytes 1572868
  70.4 8.6 %copy-start.5 = (bf16[64,64,64]{2,1,0:T(8,128)(2,1)S(1)}, bf16[64,64,64]{2,1,0:T(8,128)(2,1)}, u32[]{:S(2)}) copy-start(bf16[64,64,64]{2,1,0:T(8,128)(2,1)} %constant.208) | copy-start | bytes 1572868

commit v7 on v6

--- a/solution.py
+++ b/solution.py
@@ -178,7 +178,7 @@
 def per_device(
     coeffs, degree, material, split_coeffs, split_material, separation, reader_dev, reader_slot
 ):
-    drop_count, _, degrees, coef_width = coeffs.shape
+    drop_count, fields, degrees, coef_width = coeffs.shape
     legendre, fourier, quad_weight, normals = spectral_tables(degrees)
     nlat = legendre.shape[1]
     nlon = fourier.shape[1]
@@ -190,8 +190,11 @@
     )
     prepared = prepare(coeffs, keep_mask)
     point_weight = point_table(degrees)
+    point_weight = jnp.concatenate(
+        [point_weight, jnp.zeros(((fields - 1) * point_weight.shape[0], point_weight.shape[1]))]
+    )
     point_surface = jnp.dot(
-        (coeffs[:, 0] * keep_mask).reshape(drop_count, degrees * coef_width),
+        (coeffs * keep_mask[:, None]).reshape(drop_count, fields * degrees * coef_width),
         point_weight,
         precision=lax.Precision.DEFAULT,
     )

time: 81.3 us -> 80.9 us (level)
  other arithmetic: 6.87 us -> 8.75 us
  local copies, waits for them, and re-layouts: 18 us -> 16.8 us
  matrix products: 8.95 us -> 7.88 us
    mul x0 -> x2, other arithmetic: none -> 1.87 us  [the longest x1 1.67 us: per_device(): coeffs * keep_mask[:, None]]
    slice x1 -> x0, local copies, waits for them, and re-layouts: 1.08 us -> none  [per_device(): coeffs[:, 0] * keep_mask]
    dot_general x1, matrix products: 1.65 us -> 0.58 us  [per_device(): jnp.dot((coeffs * keep_mask[:, None]).reshape(drop_count, fields * degree...]
where the time goes in v7:
time: 80.9 us; the launch traced here: 79.6 us
  starting transfers between devices  21.2 us (26%)
  Pallas kernels  18.1 us (22%)
  local copies, waits for them, and re-layouts  16.8 us (21%)
  other arithmetic  8.75 us (11%)
  matrix products  7.88 us (10%)
  waiting for transfers between devices  5.55 us (7%)
  between operations  1.3 us (2%)
    pallas_call x1, Pallas kernels, near_field(): pl.pallas_call(functools.partial(near_kernel, points), grid=(drops,), in_...  18.1 us
    all_to_all x1, starting transfers between devices, per_device(): lax.all_to_all(jnp.broadcast_to(own_points.reshape(1, -1), (devices, drop...  11.2 us
    all_to_all x1, starting transfers between devices, per_device(): lax.all_to_all(outgoing.reshape(devices, capacity, record.shape[1]), ('ro...  10.1 us
    reshape x2, local copies, waits for them, and re-layouts, per_device(): prepared.reshape(drop_count * 4, degrees, 2, degrees)  7.52 us
    all_to_all x1, waiting for transfers between devices, per_device(): lax.all_to_all(outgoing.reshape(devices, capacity, record.shape[1]), ('ro...  5.54 us
    dot_general x1, matrix products, per_device(): jnp.einsum('mcnj,cmk->njk', batched, fourier.reshape(2, degrees, nlon), p...  2.34 us
    mul x1, other arithmetic, per_device(): coeffs * keep_mask[:, None]  1.67 us
    unnamed x43, local copies, waits for them, and re-layouts  1.63 us
  transfers between devices with their start and end apart: 3, of which 1 were waited for; matrix products, arithmetic and copies ran while one was open for 34% of the time, Pallas kernels for 23%

profile of v7, /device:TPU:0, one launch (start us, length us, event | category | flops | bytes accessed | tf_op | source)
XLA Modules:
  0.0 79.6 jit_solution(11711742876962379615)
XLA Ops:
  0.7 0.8 fusion.58
  1.5 0.2 broadcast_multiply_fusion.2
  1.7 1.7 %broadcast_multiply_fusion = bf16[16,3,64,128]{3,2,1,0:T(8,128)(2,1)S(1)} fusion(f32[16,3,64,128]{3,2,1,0:T(8,128)} %param.14, f32[16,64,128]{2,1,0:T(8,128)S(1)} %broadcast_multiply_fusion.2), kind=kLoop, calls=%fused_computation.26 | loop fusion | flops 786432 | bytes 2883584 | tf_op jit(solution)/shard_map/mul | solution.py:197
  3.4 0.6 fusion.11
  4.0 0.1 copy.169
  4.1 0.1 broadcast_in_dim.4
  4.2 0.7 broadcast_in_dim.5
  4.9 11.2 %all-to-all-start = ((bf16[128,1,64]{2,1,0:T(2,128)(2,1)}), bf16[128,1,64]{2,1,0:T(2,128)(2,1)S(1)}, u32[]{:S(2)}, u32[]{:S(2)}) async-start(bf16[128,1,64]{2,1,0:T(2,128)(2,1)} %broadcast_in_dim.5), calls=%async_computation | async-start | bytes 131072 | tf_op jit(solution)/shard_map/all_to_all | solution.py:239
  16.3 0.1 copy.211
  16.4 0.1 copy.212
  16.5 0.1 copy.210
  16.8 0.4 convolution_bitcast_fusion.2
  17.2 1.2 %fusion.68 = (bf16[16,64,128]{2,1,0:T(8,128)(2,1)}, f32[16,64,128]{2,1,0:T(8,128)}) fusion(bf16[2,64,128]{2,1,0:T(8,128)(2,1)S(1)} %copy-done.11, s32[]{:T(128)S(6)} %select_n.46, bf16[16,64,2,32]{1,0,2,3:T(8,128)(2,1)S(1)} %convolution_bitcast_fusion.2), kind=kOutput, calls=%fused_computation.115 | convolution fusion | flops 16908288 | bytes 1064964 | tf_op jit(solution)/shard_map/njw,wk->njk/dot_general | solution.py:133
  18.4 1.0 %broadcast_multiply_fusion.1 = (bf16[16,1,64,128]{3,2,1,0:T(8,128)(2,1)S(1)}, bf16[16,1,64,128]{3,2,1,0:T(8,128)(2,1)S(1)}, bf16[16,1,64,128]{3,2,1,0:T(8,128)(2,1)S(1)}, bf16[16,1,64,128]{3,2,1,0:T(8,128)(2,1)S(1)}) fusion(f32[64]{0:T(128)S(1)} %get-tuple-element.43, f32[16,64]{1,0:T(8,128)S(1)} %fusion.58, f32[64,128]{1,0:T(8,128)S(1)} %fusion.53, ...), kind=kLoop, calls=%fused_computation.45 | loop fusion | flops 1572864 | bytes 2658816 | tf_op jit(solution)/shard_map/mul | solution.py:161
  19.4 0.1 pad_maximum_fusion
  19.6 1.9 %reshape.239 = bf16[64,64,2,64]{3,2,1,0:T(2,128)(2,1)} reshape(bf16[16,4,64,128]{3,2,1,0:T(8,128)(2,1)S(1)} %pad_maximum_fusion) | data formatting | bytes 2097152 | tf_op jit(solution)/shard_map/reshape | solution.py:205
  21.4 5.7 %copy.175 = bf16[64,64,2,64]{1,0,2,3:T(8,128)(2,1)S(1)} copy(bf16[64,64,2,64]{3,2,1,0:T(2,128)(2,1)} %reshape.239) | data formatting | bytes 2097152 | tf_op jit(solution)/shard_map/reshape | solution.py:205
  27.1 0.7 fusion.69
  27.9 2.3 %fusion.2 = f32[16,4,64,128]{3,2,1,0:T(8,128)S(1)} fusion(bf16[2,64,128,1,1]{2,1,0,4,3:T(8,128)(2,1)S(1)} %copy-done.7, bf16[16,4,64,2,64]{2,1,0,3,4:T(4,128)(2,1)S(1)} %bitcast.137), kind=kOutput, calls=%fused_computation.3 | convolution fusion | flops 134217728 | bytes 3178496 | tf_op jit(solution)/shard_map/mcnj,cmk->njk/dot_general | solution.py:208
  30.2 0.3 fusion.26
  30.5 0.2 fusion.24
  30.7 0.2 copy-done.9
  31.0 0.1 reshape.246
  31.1 0.1 fusion.45
  31.2 0.2 reduce_window_sum.11
  31.3 0.2 select_reduce_fusion
  31.7 0.8 %pad_maximum_fusion.1.g_ref = bf16[16,2,64,128]{3,2,1,0:T(8,128)(2,1)} fusion(bf16[16,1,64,128]{3,2,1,0:T(8,128)(2,1)S(1)} %get-tuple-element.27, bf16[16,1,64,128]{3,2,1,0:T(8,128)(2,1)S(1)} %get-tuple-element.26), kind=kLoop, calls=%fused_computation.36 | loop fusion | flops 262144 | bytes 1048576 | tf_op jit(solution)/shard_map/stack | solution.py:235
  32.6 0.1 eq.62
  32.7 0.1 add.129
  32.8 0.1 add.130
  33.0 0.1 add.131
  33.1 0.1 mul.338
  33.3 0.1 convert_element_type.63
  33.4 0.2 reduce.1
  33.6 0.6 reshape.236
  34.2 0.4 fusion.18
  34.6 0.1 copy.171
  34.7 0.1 reshape.237
  35.1 0.2 copy.174
  35.2 0.8 %reshape.238.t_ref = f32[1408]{0:T(1024)} reshape(f32[16,8,11]{2,1,0:T(8,128)S(1)} %copy.174) | data formatting | bytes 11264 | tf_op jit(solution)/shard_map/reshape | solution.py:269
  36.0 18.1 %shard_map.157 = f32[16,4,32,128]{3,2,1,0:T(8,128)} custom-call(f32[1408]{0:T(1024)} %reshape.238.t_ref, bf16[16,2,64,128]{3,2,1,0:T(8,128)(2,1)} %pad_maximum_fusion.1.g_ref, f32[8,64,128]{2,1,0:T(8,128)} %constant.120.clone.c_ref), custom_call_target="tpu_custom_call" | custom-call | flops 100663296 | bytes 524288 | tf_op jit(solution)/shard_map/pallas_call | solution.py:402
  54.2 1.6 %reduce_sum.29 = f32[16,4,32]{2,1,0:T(4,128)S(1)} reduce(f32[16,4,32,128]{3,2,1,0:T(8,128)} %shard_map.157, f32[]{:T(128)} %constant.96.clone.1), dimensions={3}, to_apply=%region_3.4 | reduce | flops 260096 | bytes 1056772 | tf_op jit(solution)/shard_map/reduce_sum | solution.py:273
  55.9 0.1 copy.195
  56.0 0.1 reshape.248
  56.1 1.0 %fusion.41 = f32[256,13]{1,0:T(8,128)} fusion(s32[128]{0:T(128)S(1)} %multiply_add_fusion.2, f32[128,1]{0,1:T(1,128)S(1)} %convert_element_type.63, f32[128,12]{0,1:T(8,128)S(1)} %reshape.248), kind=kOutput, calls=%fused_computation.65 | convolution fusion | flops 2623104 | bytes 20480 | tf_op jit(solution)/shard_map/dot_general | solution.py:293
  57.1 10.1 %all-to-all-start.1 = ((f32[128,2,13]{2,1,0:T(2,128)}), f32[128,2,13]{2,1,0:T(2,128)S(1)}, u32[]{:S(2)}, u32[]{:S(2)}) async-start(f32[128,2,13]{2,1,0:T(2,128)} %bitcast.37), calls=%async_computation.1 | async-start | bytes 262144 | tf_op jit(solution)/shard_map/all_to_all | solution.py:294
  67.2 0.2 convolution_multiply_fusion
  67.4 0.2 reshape.241
  67.6 0.7 copy.180
  68.3 0.4 convolution_bitcast_fusion
  68.7 0.7 copy.181
  69.4 0.6 reshape.242
  70.0 1.0 %fusion.30 = f32[16,64,128]{2,1,0:T(8,128)} fusion(f32[16,64,128]{2,1,0:T(8,128)S(1)} %reshape.242, f32[16,64]{1,0:T(8,128)S(1)} %fusion.58, f32[64,128]{1,0:T(8,128)S(1)} %fusion.53), kind=kLoop, calls=%fused_computation.48 | loop fusion | flops 262144 | bytes 1085440 | tf_op jit(solution)/shard_map/mul | solution.py:309
  71.0 5.5 %all-to-all-done.1 = f32[128,2,13]{2,1,0:T(2,128)S(1)} async-done(((f32[128,2,13]{2,1,0:T(2,128)}), f32[128,2,13]{2,1,0:T(2,128)S(1)}, u32[]{:S(2)}, u32[]{:S(2)}) %all-to-all-start.1) | async-done | bytes 13344 | tf_op jit(solution)/shard_map/all_to_all | solution.py:294
  76.5 0.2 slice_reduce_fusion
  76.7 0.3 fusion.34
  77.0 0.1 copy.199
  77.1 0.7 reshape.252
  77.9 0.2 convolution_multiply_fusion.1
  78.1 0.1 reshape.244
  78.2 0.2 constant_dynamic-slice_fusion
  78.4 0.1 copy.216
  78.5 0.3 convolution_bitcast_fusion.3
  78.9 0.8 copy.200
  (71 shorter events, 1.4 us)
Async XLA Ops:
  0.6 30.9 %copy-start = (f32[256,2]{0,1:T(2,128)S(1)}, f32[256,2]{0,1:T(2,128)}, u32[]{:S(2)}) copy-start(f32[256,2]{0,1:T(2,128)} %param.18) | copy-start | bytes 6148
  0.6 2.7 %copy-start.17 = (bf16[24576,4]{0,1:T(4,128)(2,1)S(1)}, bf16[24576,4]{0,1:T(4,128)(2,1)}, u32[]{:S(2)}) copy-start(bf16[24576,4]{0,1:T(4,128)(2,1)} %constant.205) | copy-start | bytes 589828
  1.7 14.6 %copy-start.6 = (f32[4,3,64,64]{3,2,1,0:T(8,128)S(1)}, f32[4,3,64,64]{3,2,1,0:T(8,128)}, u32[]{:S(2)}) copy-start(f32[4,3,64,64]{3,2,1,0:T(8,128)} %param.17) | copy-start | bytes 589828
  3.4 13.4 %copy-start.4 = (bf16[64,64,64]{2,1,0:T(8,128)(2,1)S(1)}, bf16[64,64,64]{2,1,0:T(8,128)(2,1)}, u32[]{:S(2)}) copy-start(bf16[64,64,64]{2,1,0:T(8,128)(2,1)} %constant.209) | copy-start | bytes 1572868
  4.2 13.0 %copy-start.11 = (bf16[2,64,128]{2,1,0:T(8,128)(2,1)S(1)}, bf16[2,64,128]{2,1,0:T(8,128)(2,1)}, u32[]{:S(2)}) copy-start(bf16[2,64,128]{2,1,0:T(8,128)(2,1)} %constant.210) | copy-start | bytes 98308
  4.9 28.5 %all-to-all-start = ((bf16[128,1,64]{2,1,0:T(2,128)(2,1)}), bf16[128,1,64]{2,1,0:T(2,128)(2,1)S(1)}, u32[]{:S(2)}, u32[]{:S(2)}) async-start(bf16[128,1,64]{2,1,0:T(2,128)(2,1)} %broadcast_in_dim.5), calls=%async_computation | async-start | bytes 131072 | tf_op jit(solution)/shard_map/all_to_all | solution.py:239
  16.0 2.3 %copy-start.14 = (f32[64]{0:T(128)}, f32[64]{0:T(128)S(1)}, u32[]{:S(2)}) copy-start(f32[64]{0:T(128)S(1)} %get-tuple-element.44) | copy-start | bytes 772
  16.3 2.1 %copy-start.1 = (f32[16,3,64,128]{3,2,1,0:T(8,128)S(1)}, f32[16,3,64,128]{3,2,1,0:T(8,128)}, u32[]{:S(2)}) copy-start(f32[16,3,64,128]{3,2,1,0:T(8,128)} %param.14) | copy-start | bytes 4718596
  18.4 59.4 %collective-permute-start = (bf16[16,64,128]{2,1,0:T(8,128)(2,1)}, bf16[16,64,128]{2,1,0:T(8,128)(2,1)S(1)}, u32[]{:S(2)}, u32[]{:S(2)}) collective-permute-start(bf16[16,64,128]{2,1,0:T(8,128)(2,1)} %get-tuple-element.41), channel_id=1, source_target_pairs={{0,16},{16,0},{32,48},{48,32},{64,80},{80,64},{96,112},{112,96},{1... | collective-permute-start | bytes 786440 | tf_op jit(solution)/shard_map/ppermute | solution.py:23
  21.4 5.7 %copy-start.15 = (f32[16,2]{0,1:T(2,128)S(1)}, f32[16,2]{0,1:T(2,128)}, u32[]{:S(2)}) copy-start(f32[16,2]{0,1:T(2,128)} %param.16) | copy-start | bytes 388
  21.4 5.7 %copy-start.2 = (bf16[64,64,64,1]{2,1,3,0:T(8,128)(2,1)S(1)}, bf16[64,64,64,1]{2,1,3,0:T(8,128)(2,1)}, u32[]{:S(2)}) copy-start(bf16[64,64,64,1]{2,1,3,0:T(8,128)(2,1)} %constant.207) | copy-start | bytes 1572868
  27.1 0.8 copy-start.7
  30.2 0.7 copy-start.9
  30.2 0.8 copy-start.12
  30.5 2.1 %copy-start.10 = (f32[3,16,8]{1,2,0:T(8,128)S(1)}, f32[3,16,8]{1,2,0:T(8,128)}, u32[]{:S(2)}) copy-start(f32[3,16,8]{1,2,0:T(8,128)} %param.19) | copy-start | bytes 4612
  30.5 2.6 %copy-start.13 = (f32[3,4]{1,0:T(4,128)S(1)}, f32[3,4]{1,0:T(4,128)}, u32[]{:S(2)}) copy-start(f32[3,4]{1,0:T(4,128)} %constant.132) | copy-start | bytes 148
  36.0 31.1 %copy-start.8 = (bf16[128,128,1]{1,0,2:T(8,128)(2,1)S(1)}, bf16[128,128,1]{1,0,2:T(8,128)(2,1)}, u32[]{:S(2)}) copy-start(bf16[128,128,1]{1,0,2:T(8,128)(2,1)} %constant.208) | copy-start | bytes 98308
  36.0 31.1 %copy-start.16 = (f32[64]{0:T(128)S(1)}, f32[64]{0:T(128)}, u32[]{:S(2)}) copy-start(f32[64]{0:T(128)} %constant.117.clone) | copy-start | bytes 772
  57.1 19.5 %all-to-all-start.1 = ((f32[128,2,13]{2,1,0:T(2,128)}), f32[128,2,13]{2,1,0:T(2,128)S(1)}, u32[]{:S(2)}, u32[]{:S(2)}) async-start(f32[128,2,13]{2,1,0:T(2,128)} %bitcast.37), calls=%async_computation.1 | async-start | bytes 262144 | tf_op jit(solution)/shard_map/all_to_all | solution.py:294
  68.7 9.1 %copy-start.3 = (f32[16,64,128]{2,1,0:T(8,128)S(1)}, f32[16,64,128]{2,1,0:T(8,128)}, u32[]{:S(2)}) copy-start(f32[16,64,128]{2,1,0:T(8,128)} %get-tuple-element.42) | copy-start | bytes 1572868
  70.0 8.6 %copy-start.5 = (bf16[64,64,64]{2,1,0:T(8,128)(2,1)S(1)}, bf16[64,64,64]{2,1,0:T(8,128)(2,1)}, u32[]{:S(2)}) copy-start(bf16[64,64,64]{2,1,0:T(8,128)(2,1)} %constant.209) | copy-start | bytes 1572868
